TPU v7x, 256 devices: a whole 4x4x8 slice. The times are simulated.
256 devices in a mesh: users: 16 (over z, core), items: 16 (over y, x).
Axes of the slice: x: 4, y: 4, z: 8, core: 2. Of those that a mesh axis runs over, the one named last changes fastest.
Arguments:
- user_factors: float32 [16, 16, 512, 256], P('users', 'items'), may hold values from -0.5 to 0.5
- item_factor_blocks: float32 [16, 16, 256, 256], P('users', 'items'), may hold values from -0.5 to 0.5
- ratings: bfloat16 [16, 16, 8, 512, 256], P('users', 'items'), may hold values from -6 to 6
- rated_mask: int32 [16, 16, 8, 512, 256], P('users', 'items'), may hold values 0 or 1
- neighbor_offsets: int32 [16, 16, 4], P('users', 'items'), may hold values from -2 to 8, as said below
- neighbor_counts: int32 [16, 16], P('users', 'items'), may hold values from 1 to 4, as said below
- mix_tiles: float32 [16, 16, 4, 4, 128, 128], P('users', 'items'), may hold values from -0.5 to 0.5
- plan: int32 [8, 4], replicated, may hold values from 0 to 3, each once within a row
Outputs:
- users_out: float32 [16, 16, 512, 256], P('users', 'items')
- items_out: float32 [16, 16, 256, 256], P('users', 'items')
Inputs may be any that keep to these rules, and one draw needn't show every extreme that they name: `neighbor_offsets`: each block's list holds the four distinct offsets -2, -1, 1 and 8 in some order; only the first neighbor_counts entries are used. `neighbor_counts`: some block uses all 4 entries.
All inputs are finite; a program needn't handle non-finite values. No bound on the sum of `rated_mask` on one device may be relied on, other than what follows from the above.
Results may differ from a plain program's by a relative error of at most 0.0003.
Values sent between devices are 32-bit elements; how exact they have to be, the bound alone decides.
No kernel may reach another device: no remote copies, remote signals or barrier semaphores. Data moves between devices by JAX's collectives and lax.ppermute only.
A program may use at most 128 MiB of HBM per device.

v0:
```python
import jax
import jax.numpy as jnp
from jax import lax
from jax.sharding import PartitionSpec as P

TILE = 128
MAX_LINKS = 4
STOPS = 8
CHUNKS = 1


learning_rate = 0.025
graph_weight = 2.0
HI = lax.Precision.HIGHEST
STEP = lax.Precision.HIGH


def passed_along(value, axis, steps):
    count = lax.axis_size(axis)
    pairs = [(source, (source + steps) % count) for source in range(count)]
    return lax.ppermute(value, axis, pairs)


def chain_part(part, rows, ratings_cols, mask_cols, starts):
    errors = []
    held = []
    for k in range(len(rows)):
        block_rows = rows[k]
        rating_rows = lax.dynamic_slice_in_dim(ratings_cols, starts[k], TILE, 0).astype(jnp.float32)
        observed = lax.dynamic_slice_in_dim(mask_cols, starts[k], TILE, 0).astype(jnp.float32)
        predicted = lax.dot_general(block_rows, part, (((1,), (1,)), ((), ())), precision=STEP)
        residual_err = observed * (predicted - rating_rows)
        errors.append(residual_err)
        held.append(part)
        grad_items = lax.dot_general(
            residual_err, block_rows, (((0,), (0,)), ((), ())), precision=STEP
        )
        part = part - learning_rate * grad_items
    return part, errors, held


def graph_target(own_block, offsets, count_used, tile_collection):
    user_rows, rank_width = own_block.shape
    sub_count = user_rows // TILE
    half_span = lax.axis_size("users") // 2
    sources = ((-half_span, half_span), (2, -2), (1, -1), (-1, 1))
    neighbours = [passed_along(own_block, "users", steps) for steps, _ in sources]
    mixings = []
    for _, offset in sources:
        picked = (offsets == offset) & (jnp.arange(MAX_LINKS) < count_used)
        mixings.append(
            jnp.sum(jnp.where(picked[:, None, None, None], tile_collection, 0.0), axis=0)
        )
    mixings = lax.optimization_barrier(mixings)
    total_sum = None
    for neighbour, mixing in zip(neighbours, mixings):
        neighbour = neighbour.reshape(sub_count, TILE, rank_width)
        mixed_rows = jnp.einsum("gcj,gjz->gcz", mixing, neighbour, precision=HI)
        total_sum = mixed_rows if total_sum is None else total_sum + mixed_rows
    return total_sum.reshape(user_rows, rank_width) / count_used.astype(jnp.float32)


def shards(
    user_factors,
    item_factor_blocks,
    ratings,
    rated_mask,
    neighbor_offsets,
    neighbor_counts,
    mix_tiles,
    plan,
):
    own_block = user_factors[0, 0]
    user_rows = own_block.shape[0]
    sub_count = user_rows // TILE
    target = graph_target(own_block, neighbor_offsets[0, 0], neighbor_counts[0, 0], mix_tiles[0, 0])

    item_block = item_factor_blocks[0, 0]
    width = item_block.shape[0] // CHUNKS
    user_now = own_block
    parts = [item_block[c * width:(c + 1) * width] for c in range(CHUNKS)]
    for stop_num in range(STOPS):
        stop_ratings = ratings[0, 0, stop_num]
        halting_mask = rated_mask[0, 0, stop_num]
        starts = [plan[stop_num, k] * TILE for k in range(sub_count)]
        rows = [lax.dynamic_slice_in_dim(user_now, s, TILE, 0) for s in starts]
        last = stop_num == STOPS - 1
        errors = []
        held = []
        for c in range(CHUNKS):
            cols = slice(c * width, (c + 1) * width)
            part, errs, hs = chain_part(
                parts[c], rows, stop_ratings[:, cols], halting_mask[:, cols], starts
            )
            errors.append(errs)
            held.append(hs)
            parts[c] = part if last else passed_along(part, "items", 1)
        for k in range(sub_count):
            block_rows = rows[k]
            grad_users = graph_weight * block_rows
            if stop_num > 0:
                grad_users = grad_users - graph_weight * lax.dynamic_slice_in_dim(
                    target, starts[k], TILE, 0
                )
            for c in range(CHUNKS):
                grad_users = grad_users + jnp.dot(errors[c][k], held[c][k], precision=STEP)
            user_now = lax.dynamic_update_slice_in_dim(
                user_now, block_rows - learning_rate * grad_users, starts[k], 0
            )
        if stop_num == 0:
            user_now = user_now + (learning_rate * graph_weight) * target
    item_now = jnp.concatenate(parts, axis=0)
    return (user_now[None, None], item_now[None, None])


def solution(mesh):
    return jax.shard_map(
        shards,
        mesh=mesh,
        in_specs=(
            P("users", "items", None, None),
            P("users", "items", None, None),
            P("users", "items", None, None, None),
            P("users", "items", None, None, None),
            P("users", "items", None),
            P("users", "items"),
            P("users", "items", None, None, None, None),
            P(),
        ),
        out_specs=(P("users", "items", None, None), P("users", "items", None, None)),
        check_vma=False,
    )
```

profile of v0, /device:TPU:64, one launch (start us, length us, event | category | flops | bytes accessed | tf_op | source)
XLA Modules:
  0.0 137.3 jit_solution(17003012641583634142)
XLA Ops:
  1.2 1.9 %collective-permute-start.1 = (f32[512,256]{1,0:T(8,128)}, f32[512,256]{1,0:T(8,128)}, u32[]{:S(2)}, u32[]{:S(2)}) collective-permute-start(f32[512,256]{1,0:T(8,128)} %bitcast.449), channel_id=1, source_target_pairs={{0,32},{16,48},{32,64},{48,80},{64,96},{80,112},{96,128},{112,144}... | collective-permute-start | bytes 1572872 | tf_op jit(solution)/shard_map/ppermute | solution.py:21
  3.1 4.5 %collective-permute-start = (f32[512,256]{1,0:T(8,128)}, f32[512,256]{1,0:T(8,128)}, u32[]{:S(2)}, u32[]{:S(2)}) collective-permute-start(f32[512,256]{1,0:T(8,128)} %bitcast.450), channel_id=1, source_target_pairs={{0,128},{16,144},{32,160},{48,176},{64,192},{80,208},{96,224},{112... | collective-permute-start | bytes 1572872 | tf_op jit(solution)/shard_map/ppermute | solution.py:21
  7.6 1.8 %fusion.313 = (s32[1,1]{0,1:T(1,128)}, s32[1,1]{0,1:T(1,128)}, s32[1,1]{0,1:T(1,128)}, s32[1,1]{0,1:T(1,128)}, s32[1,1]{0,1:T(1,128)}, /*index=5*/s32[1,1]{0,1:T...) fusion(s32[8,4]{0,1:T(4,128)} %param.15), kind=kLoop, calls=%fused_computation.424 | loop fusion | bytes 104 | tf_op jit(solution)/shard_map/slice | solution.py:85
  12.1 2.9 %fusion.311 = (bf16[1,1,1,512,256]{4,3,2,1,0:T(8,128)(2,1)}, bf16[1,1,1,512,256]{4,3,2,1,0:T(8,128)(2,1)}, bf16[1,1,1,512,256]{4,3,2,1,0:T(8,128)(2,1)}, bf16[1,...) fusion(bf16[1,1,8,512,256]{4,3,2,1,0:T(8,128)(2,1)} %param.10), kind=kLoop, calls=%fused_computation.422 | loop fusion | bytes 4194304 | tf_op jit(solution)/shard_map/slice | solution.py:83
  15.3 1.5 %fusion.310 = (s32[1,1,1,512,256]{4,3,2,1,0:T(8,128)S(1)}, s32[1,1,1,512,256]{4,3,2,1,0:T(8,128)}, s32[1,1,1,512,256]{4,3,2,1,0:T(8,128)}, s32[1,1,1,512,256]{4,...) fusion(s32[1,1,8,512,256]{4,3,2,1,0:T(8,128)S(1)} %copy-done.1), kind=kLoop, calls=%fused_computation.421 | loop fusion | bytes 8388608 | tf_op jit(solution)/shard_map/slice | solution.py:84
  18.9 1.2 fusion.155
  20.2 1.0 fusion.32
  21.2 1.5 %collective-permute-start.4 = (f32[256,256]{1,0:T(8,128)}, f32[256,256]{1,0:T(8,128)S(1)}, u32[]{:S(2)}, u32[]{:S(2)}) collective-permute-start(f32[256,256]{1,0:T(8,128)} %fusion.32), channel_id=1, source_target_pairs={{0,1},{1,2},{2,3},{3,4},{4,5},{5,6},{6,7},{7,8},{8,9},{9,10},{10,1... | collective-permute-start | bytes 786440 | tf_op jit(solution)/shard_map/ppermute | solution.py:21
  23.6 1.1 fusion.162
  24.8 1.1 fusion.158
  26.6 0.7 fusion.312
  45.1 1.6 %fusion.316 = f32[4,128,256]{2,1,0:T(8,128)S(1)} fusion(f32[4,128,128]{2,1,0:T(8,128)S(1)} %get-tuple-element.9, f32[4,128,256]{2,1,0:T(8,128)} %bitcast.27), kind=kOutput, calls=%fused_computation.427 | convolution fusion | flops 201326592 | bytes 1310720 | tf_op jit(solution)/shard_map/gcj,gjz->gcz/dot_general | solution.py:58
  46.8 1.7 %fusion.315 = f32[4,128,256]{2,1,0:T(8,128)S(1)} fusion(f32[4,128,128]{2,1,0:T(8,128)S(1)} %get-tuple-element.8, f32[4,128,256]{2,1,0:T(8,128)} %bitcast.26), kind=kOutput, calls=%fused_computation.426 | convolution fusion | flops 201326592 | bytes 1310720 | tf_op jit(solution)/shard_map/gcj,gjz->gcz/dot_general | solution.py:58
  48.5 1.6 %fusion.314 = f32[4,128,256]{2,1,0:T(8,128)S(1)} fusion(f32[4,128,128]{2,1,0:T(8,128)S(1)} %get-tuple-element.7, f32[4,128,256]{2,1,0:T(8,128)} %bitcast.25), kind=kOutput, calls=%fused_computation.425 | convolution fusion | flops 201326592 | bytes 1310720 | tf_op jit(solution)/shard_map/gcj,gjz->gcz/dot_general | solution.py:58
  50.1 1.7 %fusion.2 = f32[4,128,256]{2,1,0:T(8,128)S(1)} fusion(f32[4,128,256]{2,1,0:T(8,128)S(1)} %fusion.316, f32[4,128,256]{2,1,0:T(8,128)S(1)} %fusion.315, f32[4,128,256]{2,1,0:T(8,128)S(1)} %fusion.314, f32[4,128,128]{2,1,0:T(8,128)S(1)} %get-tuple-element.6, f32[4,128,256]{2,1,0:T(8,128)} %bitcast.24, f32[]{:T(128)S(6)} %convert_element_type.403), kind=kOutput, calls=%fused_computation.3 | convolution fusion | flops 201850880 | bytes 2883588 | tf_op jit(solution)/shard_map/gcj,gjz->gcz/dot_general | solution.py:58
  54.5 1.7 %collective-permute-start.5 = (f32[256,256]{1,0:T(8,128)S(1)}, f32[256,256]{1,0:T(8,128)S(1)}, u32[]{:S(2)}, u32[]{:S(2)}) collective-permute-start(f32[256,256]{1,0:T(8,128)S(1)} %fusion.28), channel_id=1, source_target_pairs={{0,1},{1,2},{2,3},{3,4},{4,5},{5,6},{6,7},{7,8},{8,9},{9,10},{10,1... | collective-permute-start | bytes 786440 | tf_op jit(solution)/shard_map/ppermute | solution.py:21
  57.3 9.6 %collective-permute-done.5 = f32[256,256]{1,0:T(8,128)S(1)} collective-permute-done((f32[256,256]{1,0:T(8,128)S(1)}, f32[256,256]{1,0:T(8,128)S(1)}, u32[]{:S(2)}, u32[]{:S(2)}) %collective-permute-start.5) | collective-permute-done | bytes 262176 | tf_op jit(solution)/shard_map/ppermute | solution.py:21
  70.6 10.7 %collective-permute-done.6 = f32[256,256]{1,0:T(8,128)S(1)} collective-permute-done((f32[256,256]{1,0:T(8,128)S(1)}, f32[256,256]{1,0:T(8,128)S(1)}, u32[]{:S(2)}, u32[]{:S(2)}) %collective-permute-start.6) | collective-permute-done | bytes 262176 | tf_op jit(solution)/shard_map/ppermute | solution.py:21
  84.9 9.9 %collective-permute-done.7 = f32[256,256]{1,0:T(8,128)S(1)} collective-permute-done((f32[256,256]{1,0:T(8,128)S(1)}, f32[256,256]{1,0:T(8,128)S(1)}, u32[]{:S(2)}, u32[]{:S(2)}) %collective-permute-start.7) | collective-permute-done | bytes 262176 | tf_op jit(solution)/shard_map/ppermute | solution.py:21
  98.5 8.9 %collective-permute-done.8 = f32[256,256]{1,0:T(8,128)S(1)} collective-permute-done((f32[256,256]{1,0:T(8,128)S(1)}, f32[256,256]{1,0:T(8,128)S(1)}, u32[]{:S(2)}, u32[]{:S(2)}) %collective-permute-start.8) | collective-permute-done | bytes 262176 | tf_op jit(solution)/shard_map/ppermute | solution.py:21
  111.3 8.6 %collective-permute-done.9 = f32[256,256]{1,0:T(8,128)S(1)} collective-permute-done((f32[256,256]{1,0:T(8,128)S(1)}, f32[256,256]{1,0:T(8,128)S(1)}, u32[]{:S(2)}, u32[]{:S(2)}) %collective-permute-start.9) | collective-permute-done | bytes 262176 | tf_op jit(solution)/shard_map/ppermute | solution.py:21
  123.7 8.6 %collective-permute-done.10 = f32[256,256]{1,0:T(8,128)S(1)} collective-permute-done((f32[256,256]{1,0:T(8,128)S(1)}, f32[256,256]{1,0:T(8,128)S(1)}, u32[]{:S(2)}, u32[]{:S(2)}) %collective-permute-start.10) | collective-permute-done | bytes 262176 | tf_op jit(solution)/shard_map/ppermute | solution.py:21
  134.5 1.0 fusion.4
  136.5 0.8 copy-done.19
  (157 shorter events, 28.6 us)
Async XLA Ops:
  0.6 44.5 %collective-permute-start.3 = (f32[512,256]{1,0:T(8,128)}, f32[512,256]{1,0:T(8,128)}, u32[]{:S(2)}, u32[]{:S(2)}) collective-permute-start(f32[512,256]{1,0:T(8,128)} %bitcast.447), channel_id=1, source_target_pairs={{0,240},{16,0},{32,16},{48,32},{64,48},{80,64},{96,80},{112,96},{1... | collective-permute-start | bytes 1572872 | tf_op jit(solution)/shard_map/ppermute | solution.py:21
  0.7 46.1 %collective-permute-start.2 = (f32[512,256]{1,0:T(8,128)}, f32[512,256]{1,0:T(8,128)}, u32[]{:S(2)}, u32[]{:S(2)}) collective-permute-start(f32[512,256]{1,0:T(8,128)} %bitcast.448), channel_id=1, source_target_pairs={{0,16},{16,32},{32,48},{48,64},{64,80},{80,96},{96,112},{112,128},... | collective-permute-start | bytes 1572872 | tf_op jit(solution)/shard_map/ppermute | solution.py:21
  1.2 47.3 %collective-permute-start.1 = (f32[512,256]{1,0:T(8,128)}, f32[512,256]{1,0:T(8,128)}, u32[]{:S(2)}, u32[]{:S(2)}) collective-permute-start(f32[512,256]{1,0:T(8,128)} %bitcast.449), channel_id=1, source_target_pairs={{0,32},{16,48},{32,64},{48,80},{64,96},{80,112},{96,128},{112,144}... | collective-permute-start | bytes 1572872 | tf_op jit(solution)/shard_map/ppermute | solution.py:21
  3.1 47.1 %collective-permute-start = (f32[512,256]{1,0:T(8,128)}, f32[512,256]{1,0:T(8,128)}, u32[]{:S(2)}, u32[]{:S(2)}) collective-permute-start(f32[512,256]{1,0:T(8,128)} %bitcast.450), channel_id=1, source_target_pairs={{0,128},{16,144},{32,160},{48,176},{64,192},{80,208},{96,224},{112... | collective-permute-start | bytes 1572872 | tf_op jit(solution)/shard_map/ppermute | solution.py:21
  17.6 8.6 %copy-start.21 = (s32[1,1,4]{2,1,0:T(1,128)S(1)}, s32[1,1,4]{2,1,0:T(1,128)}, u32[]{:S(2)}) copy-start(s32[1,1,4]{2,1,0:T(1,128)} %param.12) | copy-start | bytes 52
  18.6 8.0 %copy-start.20 = (s32[8,4]{0,1:T(4,128)S(1)}, s32[8,4]{0,1:T(4,128)}, u32[]{:S(2)}) copy-start(s32[8,4]{0,1:T(4,128)} %param.15) | copy-start | bytes 388
  18.9 7.3 %copy-start.10 = (f32[1,1,4,4,128,128]{5,4,3,2,1,0:T(8,128)S(1)}, f32[1,1,4,4,128,128]{5,4,3,2,1,0:T(8,128)}, u32[]{:S(2)}) copy-start(f32[1,1,4,4,128,128]{5,4,3,2,1,0:T(8,128)} %param.14) | copy-start | bytes 3145732
  21.2 30.7 %collective-permute-start.4 = (f32[256,256]{1,0:T(8,128)}, f32[256,256]{1,0:T(8,128)S(1)}, u32[]{:S(2)}, u32[]{:S(2)}) collective-permute-start(f32[256,256]{1,0:T(8,128)} %fusion.32), channel_id=1, source_target_pairs={{0,1},{1,2},{2,3},{3,4},{4,5},{5,6},{6,7},{7,8},{8,9},{9,10},{10,1... | collective-permute-start | bytes 786440 | tf_op jit(solution)/shard_map/ppermute | solution.py:21
  52.6 14.3 %copy-start.6 = (s32[1,1,1,512,256]{4,3,2,1,0:T(8,128)S(1)}, s32[1,1,1,512,256]{4,3,2,1,0:T(8,128)}, u32[]{:S(2)}) copy-start(s32[1,1,1,512,256]{4,3,2,1,0:T(8,128)} %get-tuple-element.18) | copy-start | bytes 1572868
  52.6 14.3 %copy-start.16 = (bf16[1,1,1,512,256]{4,3,2,1,0:T(8,128)(2,1)S(1)}, bf16[1,1,1,512,256]{4,3,2,1,0:T(8,128)(2,1)}, u32[]{:S(2)}) copy-start(bf16[1,1,1,512,256]{4,3,2,1,0:T(8,128)(2,1)} %get-tuple-element.26) | copy-start | bytes 786436
  54.5 12.4 %collective-permute-start.5 = (f32[256,256]{1,0:T(8,128)S(1)}, f32[256,256]{1,0:T(8,128)S(1)}, u32[]{:S(2)}, u32[]{:S(2)}) collective-permute-start(f32[256,256]{1,0:T(8,128)S(1)} %fusion.28), channel_id=1, source_target_pairs={{0,1},{1,2},{2,3},{3,4},{4,5},{5,6},{6,7},{7,8},{8,9},{9,10},{10,1... | collective-permute-start | bytes 786440 | tf_op jit(solution)/shard_map/ppermute | solution.py:21
  67.5 13.7 %copy-start.5 = (s32[1,1,1,512,256]{4,3,2,1,0:T(8,128)S(1)}, s32[1,1,1,512,256]{4,3,2,1,0:T(8,128)}, u32[]{:S(2)}) copy-start(s32[1,1,1,512,256]{4,3,2,1,0:T(8,128)} %get-tuple-element.17) | copy-start | bytes 1572868
  67.5 13.7 %copy-start.15 = (bf16[1,1,1,512,256]{4,3,2,1,0:T(8,128)(2,1)S(1)}, bf16[1,1,1,512,256]{4,3,2,1,0:T(8,128)(2,1)}, u32[]{:S(2)}) copy-start(bf16[1,1,1,512,256]{4,3,2,1,0:T(8,128)(2,1)} %get-tuple-element.25) | copy-start | bytes 786436
  69.4 11.8 %collective-permute-start.6 = (f32[256,256]{1,0:T(8,128)S(1)}, f32[256,256]{1,0:T(8,128)S(1)}, u32[]{:S(2)}, u32[]{:S(2)}) collective-permute-start(f32[256,256]{1,0:T(8,128)S(1)} %fusion.24), channel_id=1, source_target_pairs={{0,1},{1,2},{2,3},{3,4},{4,5},{5,6},{6,7},{7,8},{8,9},{9,10},{10,1... | collective-permute-start | bytes 786440 | tf_op jit(solution)/shard_map/ppermute | solution.py:21
  81.9 12.9 %copy-start.4 = (s32[1,1,1,512,256]{4,3,2,1,0:T(8,128)S(1)}, s32[1,1,1,512,256]{4,3,2,1,0:T(8,128)}, u32[]{:S(2)}) copy-start(s32[1,1,1,512,256]{4,3,2,1,0:T(8,128)} %get-tuple-element.16) | copy-start | bytes 1572868
  81.9 12.9 %copy-start.14 = (bf16[1,1,1,512,256]{4,3,2,1,0:T(8,128)(2,1)S(1)}, bf16[1,1,1,512,256]{4,3,2,1,0:T(8,128)(2,1)}, u32[]{:S(2)}) copy-start(bf16[1,1,1,512,256]{4,3,2,1,0:T(8,128)(2,1)} %get-tuple-element.24) | copy-start | bytes 786436
  83.8 11.0 %collective-permute-start.7 = (f32[256,256]{1,0:T(8,128)S(1)}, f32[256,256]{1,0:T(8,128)S(1)}, u32[]{:S(2)}, u32[]{:S(2)}) collective-permute-start(f32[256,256]{1,0:T(8,128)S(1)} %fusion.20), channel_id=1, source_target_pairs={{0,1},{1,2},{2,3},{3,4},{4,5},{5,6},{6,7},{7,8},{8,9},{9,10},{10,1... | collective-permute-start | bytes 786440 | tf_op jit(solution)/shard_map/ppermute | solution.py:21
  95.4 12.0 %copy-start.3 = (s32[1,1,1,512,256]{4,3,2,1,0:T(8,128)S(1)}, s32[1,1,1,512,256]{4,3,2,1,0:T(8,128)}, u32[]{:S(2)}) copy-start(s32[1,1,1,512,256]{4,3,2,1,0:T(8,128)} %get-tuple-element.15) | copy-start | bytes 1572868
  95.5 12.0 %copy-start.13 = (bf16[1,1,1,512,256]{4,3,2,1,0:T(8,128)(2,1)S(1)}, bf16[1,1,1,512,256]{4,3,2,1,0:T(8,128)(2,1)}, u32[]{:S(2)}) copy-start(bf16[1,1,1,512,256]{4,3,2,1,0:T(8,128)(2,1)} %get-tuple-element.23) | copy-start | bytes 786436
  97.4 10.1 %collective-permute-start.8 = (f32[256,256]{1,0:T(8,128)S(1)}, f32[256,256]{1,0:T(8,128)S(1)}, u32[]{:S(2)}, u32[]{:S(2)}) collective-permute-start(f32[256,256]{1,0:T(8,128)S(1)} %fusion.16), channel_id=1, source_target_pairs={{0,1},{1,2},{2,3},{3,4},{4,5},{5,6},{6,7},{7,8},{8,9},{9,10},{10,1... | collective-permute-start | bytes 786440 | tf_op jit(solution)/shard_map/ppermute | solution.py:21
  108.1 11.9 %copy-start.12 = (bf16[1,1,1,512,256]{4,3,2,1,0:T(8,128)(2,1)S(1)}, bf16[1,1,1,512,256]{4,3,2,1,0:T(8,128)(2,1)}, u32[]{:S(2)}) copy-start(bf16[1,1,1,512,256]{4,3,2,1,0:T(8,128)(2,1)} %get-tuple-element.29) | copy-start | bytes 786436
  110.0 10.0 %collective-permute-start.9 = (f32[256,256]{1,0:T(8,128)S(1)}, f32[256,256]{1,0:T(8,128)S(1)}, u32[]{:S(2)}, u32[]{:S(2)}) collective-permute-start(f32[256,256]{1,0:T(8,128)S(1)} %fusion.12), channel_id=1, source_target_pairs={{0,1},{1,2},{2,3},{3,4},{4,5},{5,6},{6,7},{7,8},{8,9},{9,10},{10,1... | collective-permute-start | bytes 786440 | tf_op jit(solution)/shard_map/ppermute | solution.py:21
  120.6 11.7 %copy-start.11 = (bf16[1,1,1,512,256]{4,3,2,1,0:T(8,128)(2,1)S(1)}, bf16[1,1,1,512,256]{4,3,2,1,0:T(8,128)(2,1)}, u32[]{:S(2)}) copy-start(bf16[1,1,1,512,256]{4,3,2,1,0:T(8,128)(2,1)} %get-tuple-element.22) | copy-start | bytes 786436
  122.5 9.8 %collective-permute-start.10 = (f32[256,256]{1,0:T(8,128)S(1)}, f32[256,256]{1,0:T(8,128)S(1)}, u32[]{:S(2)}, u32[]{:S(2)}) collective-permute-start(f32[256,256]{1,0:T(8,128)S(1)} %fusion.8), channel_id=1, source_target_pairs={{0,1},{1,2},{2,3},{3,4},{4,5},{5,6},{6,7},{7,8},{8,9},{9,10},{10,1... | collective-permute-start | bytes 786440 | tf_op jit(solution)/shard_map/ppermute | solution.py:21
  (9 other events, 26.4 us)
where the time goes:
time: 138 us; the launch traced here: 137 us
  waiting for transfers between devices  56.4 us (41%)
  matrix products  38.2 us (28%)
  between operations  22.9 us (17%)
  starting transfers between devices  10.8 us (8%)
  local copies, waits for them, and re-layouts  8.65 us (6%)
    ppermute x11, waiting for transfers between devices, passed_along(): return lax.ppermute(value, axis, pairs)  56.4 us
    dot_general x32, matrix products, chain_part(): lax.dot_general(residual_err, block_rows, (((0,), (0,)), ((), ())), preci...  11.3 us
    ppermute x11, starting transfers between devices, passed_along(): return lax.ppermute(value, axis, pairs)  10.8 us
    dot_general x32, matrix products, chain_part(): lax.dot_general(block_rows, part, (((1,), (1,)), ((), ())), precision=STEP)  10.7 us
    dot_general x32, matrix products, shards(): grad_users = grad_users + jnp.dot(errors[c][k], held[c][k], precision=STEP)  9.56 us
    dot_general x4, matrix products, graph_target(): mixed_rows = jnp.einsum('gcj,gjz->gcz', mixing, neighbour, precision=HI)  6.6 us
    slice x1, local copies, waits for them, and re-layouts, shards(): stop_ratings = ratings[0, 0, stop_num]  2.89 us
  transfers between devices with their start and end apart: 11, of which 6 were waited for; matrix products, arithmetic and copies ran while one was open for 20% of the time, Pallas kernels for 0%

commit v1 on v0

--- a/solution.py
+++ b/solution.py
@@ -51,12 +51,8 @@
         mixings.append(
             jnp.sum(jnp.where(picked[:, None, None, None], tile_collection, 0.0), axis=0)
         )
-    mixings = lax.optimization_barrier(mixings)
-    total_sum = None
-    for neighbour, mixing in zip(neighbours, mixings):
-        neighbour = neighbour.reshape(sub_count, TILE, rank_width)
-        mixed_rows = jnp.einsum("gcj,gjz->gcz", mixing, neighbour, precision=HI)
-        total_sum = mixed_rows if total_sum is None else total_sum + mixed_rows
+    stacked = jnp.stack(neighbours).reshape(len(sources), sub_count, TILE, rank_width)
+    total_sum = jnp.einsum("bgcj,bgjz->gcz", jnp.stack(mixings), stacked, precision=STEP)
     return total_sum.reshape(user_rows, rank_width) / count_used.astype(jnp.float32)
 
 

time: 138 us -> 137 us (level)
  the two profiles are of different devices: /device:TPU:64 before, /device:TPU:0 now
where the time goes in v1:
time: 137 us; the launch traced here: 136 us
  waiting for transfers between devices  58.1 us (42%)
  matrix products  33.2 us (24%)
  between operations  22.8 us (17%)
  starting transfers between devices  10.9 us (8%)
  local copies, waits for them, and re-layouts  9.63 us (7%)
    ppermute x11, waiting for transfers between devices, passed_along(): return lax.ppermute(value, axis, pairs)  58.1 us
    dot_general x32, matrix products, chain_part(): lax.dot_general(residual_err, block_rows, (((0,), (0,)), ((), ())), preci...  11.4 us
    ppermute x11, starting transfers between devices, passed_along(): return lax.ppermute(value, axis, pairs)  10.9 us
    dot_general x32, matrix products, chain_part(): lax.dot_general(block_rows, part, (((1,), (1,)), ((), ())), precision=STEP)  10.7 us
    dot_general x32, matrix products, shards(): grad_users = grad_users + jnp.dot(errors[c][k], held[c][k], precision=STEP)  8.67 us
    slice x1, local copies, waits for them, and re-layouts, shards(): stop_ratings = ratings[0, 0, stop_num]  2.9 us
  transfers between devices with their start and end apart: 11, of which 6 were waited for; matrix products, arithmetic and copies ran while one was open for 17% of the time, Pallas kernels for 0%

profile of v1, /device:TPU:0, one launch (start us, length us, event | category | flops | bytes accessed | tf_op | source)
XLA Modules:
  0.0 135.9 jit_solution(7403926607393771851)
XLA Ops:
  0.6 3.6 %collective-permute-start.3 = (f32[512,256]{1,0:T(8,128)}, f32[512,256]{1,0:T(8,128)}, u32[]{:S(2)}, u32[]{:S(2)}) collective-permute-start(f32[512,256]{1,0:T(8,128)} %bitcast.456), channel_id=1, source_target_pairs={{0,240},{16,0},{32,16},{48,32},{64,48},{80,64},{96,80},{112,96},{1... | collective-permute-start | bytes 1572872 | tf_op jit(solution)/shard_map/ppermute | solution.py:21
  4.2 3.4 %collective-permute-start = (f32[512,256]{1,0:T(8,128)}, f32[512,256]{1,0:T(8,128)}, u32[]{:S(2)}, u32[]{:S(2)}) collective-permute-start(f32[512,256]{1,0:T(8,128)} %bitcast.459), channel_id=1, source_target_pairs={{0,128},{16,144},{32,160},{48,176},{64,192},{80,208},{96,224},{112... | collective-permute-start | bytes 1572872 | tf_op jit(solution)/shard_map/ppermute | solution.py:21
  7.6 1.8 %fusion.334 = (s32[1,1]{0,1:T(1,128)}, s32[1,1]{0,1:T(1,128)}, s32[1,1]{0,1:T(1,128)}, s32[1,1]{0,1:T(1,128)}, s32[1,1]{0,1:T(1,128)}, /*index=5*/s32[1,1]{0,1:T...) fusion(s32[8,4]{0,1:T(4,128)} %param.15), kind=kLoop, calls=%fused_computation.438 | loop fusion | bytes 104 | tf_op jit(solution)/shard_map/slice | solution.py:81
  12.1 2.9 %fusion.332 = (bf16[1,1,1,512,256]{4,3,2,1,0:T(8,128)(2,1)}, bf16[1,1,1,512,256]{4,3,2,1,0:T(8,128)(2,1)}, bf16[1,1,1,512,256]{4,3,2,1,0:T(8,128)(2,1)}, bf16[1,...) fusion(bf16[1,1,8,512,256]{4,3,2,1,0:T(8,128)(2,1)} %param.10), kind=kLoop, calls=%fused_computation.436 | loop fusion | bytes 4194304 | tf_op jit(solution)/shard_map/slice | solution.py:79
  15.0 0.4 copy-done.1
  15.3 1.5 %fusion.331 = (s32[1,1,1,512,256]{4,3,2,1,0:T(8,128)S(1)}, s32[1,1,1,512,256]{4,3,2,1,0:T(8,128)}, s32[1,1,1,512,256]{4,3,2,1,0:T(8,128)}, s32[1,1,1,512,256]{4,...) fusion(s32[1,1,8,512,256]{4,3,2,1,0:T(8,128)S(1)} %copy-done.1), kind=kLoop, calls=%fused_computation.435 | loop fusion | bytes 8388608 | tf_op jit(solution)/shard_map/slice | solution.py:80
  19.0 1.2 fusion.163
  20.2 1.0 fusion.40
  21.3 1.5 %collective-permute-start.4 = (f32[256,256]{1,0:T(8,128)}, f32[256,256]{1,0:T(8,128)S(1)}, u32[]{:S(2)}, u32[]{:S(2)}) collective-permute-start(f32[256,256]{1,0:T(8,128)} %fusion.40), channel_id=1, source_target_pairs={{0,1},{1,2},{2,3},{3,4},{4,5},{5,6},{6,7},{7,8},{8,9},{9,10},{10,1... | collective-permute-start | bytes 786440 | tf_op jit(solution)/shard_map/ppermute | solution.py:21
  23.7 1.2 fusion.170
  24.9 1.3 fusion.183
  26.2 0.7 fusion.333
  45.3 2.5 %fusion.187 = f32[4,128,256]{2,1,0:T(8,128)S(1)} fusion(f32[1,4,128,256]{3,2,0,1:T(8,128)} %bitcast.35, f32[1,4,128,256]{3,2,0,1:T(8,128)} %bitcast.33, f32[1,4,128,256]{3,2,0,1:T(8,128)} %bitcast.31, f32[1,4,128,256]{3,2,0,1:T(8,128)} %bitcast.29, f32[1,4,128,128]{3,2,0,1:T(8,128)} %bitcast.464, f32[1,4,128,128]{3,2,0,1:T(8,128)} %bitcast.463, ...), kind=kOutput, calls=%fused_computation.286 | convolution fusion | flops 405143552 | bytes 3670020 | tf_op jit(solution)/shard_map/bgcj,bgjz->gcz/dot_general | solution.py:55
  47.9 0.9 copy-done.7
  51.4 1.6 %collective-permute-start.5 = (f32[256,256]{1,0:T(8,128)S(1)}, f32[256,256]{1,0:T(8,128)S(1)}, u32[]{:S(2)}, u32[]{:S(2)}) collective-permute-start(f32[256,256]{1,0:T(8,128)S(1)} %fusion.36), channel_id=1, source_target_pairs={{0,1},{1,2},{2,3},{3,4},{4,5},{5,6},{6,7},{7,8},{8,9},{9,10},{10,1... | collective-permute-start | bytes 786440 | tf_op jit(solution)/shard_map/ppermute | solution.py:21
  54.0 8.0 %collective-permute-done.5 = f32[256,256]{1,0:T(8,128)S(1)} collective-permute-done((f32[256,256]{1,0:T(8,128)S(1)}, f32[256,256]{1,0:T(8,128)S(1)}, u32[]{:S(2)}, u32[]{:S(2)}) %collective-permute-start.5) | collective-permute-done | bytes 262176 | tf_op jit(solution)/shard_map/ppermute | solution.py:21
  65.9 10.7 %collective-permute-done.6 = f32[256,256]{1,0:T(8,128)S(1)} collective-permute-done((f32[256,256]{1,0:T(8,128)S(1)}, f32[256,256]{1,0:T(8,128)S(1)}, u32[]{:S(2)}, u32[]{:S(2)}) %collective-permute-start.6) | collective-permute-done | bytes 262176 | tf_op jit(solution)/shard_map/ppermute | solution.py:21
  80.3 11.1 %collective-permute-done.7 = f32[256,256]{1,0:T(8,128)S(1)} collective-permute-done((f32[256,256]{1,0:T(8,128)S(1)}, f32[256,256]{1,0:T(8,128)S(1)}, u32[]{:S(2)}, u32[]{:S(2)}) %collective-permute-start.7) | collective-permute-done | bytes 262176 | tf_op jit(solution)/shard_map/ppermute | solution.py:21
  95.0 10.3 %collective-permute-done.8 = f32[256,256]{1,0:T(8,128)S(1)} collective-permute-done((f32[256,256]{1,0:T(8,128)S(1)}, f32[256,256]{1,0:T(8,128)S(1)}, u32[]{:S(2)}, u32[]{:S(2)}) %collective-permute-start.8) | collective-permute-done | bytes 262176 | tf_op jit(solution)/shard_map/ppermute | solution.py:21
  109.2 9.4 %collective-permute-done.9 = f32[256,256]{1,0:T(8,128)S(1)} collective-permute-done((f32[256,256]{1,0:T(8,128)S(1)}, f32[256,256]{1,0:T(8,128)S(1)}, u32[]{:S(2)}, u32[]{:S(2)}) %collective-permute-start.9) | collective-permute-done | bytes 262176 | tf_op jit(solution)/shard_map/ppermute | solution.py:21
  122.3 8.6 %collective-permute-done.10 = f32[256,256]{1,0:T(8,128)S(1)} collective-permute-done((f32[256,256]{1,0:T(8,128)S(1)}, f32[256,256]{1,0:T(8,128)S(1)}, u32[]{:S(2)}, u32[]{:S(2)}) %collective-permute-start.10) | collective-permute-done | bytes 262176 | tf_op jit(solution)/shard_map/ppermute | solution.py:21
  131.9 0.3 fusion.14
  133.1 1.0 fusion.12
  135.2 0.8 copy-done.22
  (160 shorter events, 27.4 us)
Async XLA Ops:
  0.6 44.6 %collective-permute-start.3 = (f32[512,256]{1,0:T(8,128)}, f32[512,256]{1,0:T(8,128)}, u32[]{:S(2)}, u32[]{:S(2)}) collective-permute-start(f32[512,256]{1,0:T(8,128)} %bitcast.456), channel_id=1, source_target_pairs={{0,240},{16,0},{32,16},{48,32},{64,48},{80,64},{96,80},{112,96},{1... | collective-permute-start | bytes 1572872 | tf_op jit(solution)/shard_map/ppermute | solution.py:21
  4.2 41.0 %collective-permute-start.2 = (f32[512,256]{1,0:T(8,128)}, f32[512,256]{1,0:T(8,128)}, u32[]{:S(2)}, u32[]{:S(2)}) collective-permute-start(f32[512,256]{1,0:T(8,128)} %bitcast.457), channel_id=1, source_target_pairs={{0,16},{16,32},{32,48},{48,64},{64,80},{80,96},{96,112},{112,128},... | collective-permute-start | bytes 1572872 | tf_op jit(solution)/shard_map/ppermute | solution.py:21
  4.2 41.0 %collective-permute-start.1 = (f32[512,256]{1,0:T(8,128)}, f32[512,256]{1,0:T(8,128)}, u32[]{:S(2)}, u32[]{:S(2)}) collective-permute-start(f32[512,256]{1,0:T(8,128)} %bitcast.458), channel_id=1, source_target_pairs={{0,32},{16,48},{32,64},{48,80},{64,96},{80,112},{96,128},{112,144}... | collective-permute-start | bytes 1572872 | tf_op jit(solution)/shard_map/ppermute | solution.py:21
  4.2 41.0 %collective-permute-start = (f32[512,256]{1,0:T(8,128)}, f32[512,256]{1,0:T(8,128)}, u32[]{:S(2)}, u32[]{:S(2)}) collective-permute-start(f32[512,256]{1,0:T(8,128)} %bitcast.459), channel_id=1, source_target_pairs={{0,128},{16,144},{32,160},{48,176},{64,192},{80,208},{96,224},{112... | collective-permute-start | bytes 1572872 | tf_op jit(solution)/shard_map/ppermute | solution.py:21
  18.9 6.0 %copy-start.24 = (s32[1,1,4]{2,1,0:T(1,128)S(1)}, s32[1,1,4]{2,1,0:T(1,128)}, u32[]{:S(2)}) copy-start(s32[1,1,4]{2,1,0:T(1,128)} %param.12) | copy-start | bytes 52
  19.0 6.0 %copy-start.13 = (f32[1,1,4,4,128,128]{5,4,3,2,1,0:T(8,128)S(1)}, f32[1,1,4,4,128,128]{5,4,3,2,1,0:T(8,128)}, u32[]{:S(2)}) copy-start(f32[1,1,4,4,128,128]{5,4,3,2,1,0:T(8,128)} %param.14) | copy-start | bytes 3145732
  21.3 26.7 %collective-permute-start.4 = (f32[256,256]{1,0:T(8,128)}, f32[256,256]{1,0:T(8,128)S(1)}, u32[]{:S(2)}, u32[]{:S(2)}) collective-permute-start(f32[256,256]{1,0:T(8,128)} %fusion.40), channel_id=1, source_target_pairs={{0,1},{1,2},{2,3},{3,4},{4,5},{5,6},{6,7},{7,8},{8,9},{9,10},{10,1... | collective-permute-start | bytes 786440 | tf_op jit(solution)/shard_map/ppermute | solution.py:21
  23.7 21.3 %copy-start.9 = (f32[128,256]{1,0:T(8,128)S(1)}, f32[128,256]{1,0:T(8,128)}, u32[]{:S(2)}) copy-start(f32[128,256]{1,0:T(8,128)} %copy-done.8) | copy-start | bytes 393220
  51.4 10.6 %collective-permute-start.5 = (f32[256,256]{1,0:T(8,128)S(1)}, f32[256,256]{1,0:T(8,128)S(1)}, u32[]{:S(2)}, u32[]{:S(2)}) collective-permute-start(f32[256,256]{1,0:T(8,128)S(1)} %fusion.36), channel_id=1, source_target_pairs={{0,1},{1,2},{2,3},{3,4},{4,5},{5,6},{6,7},{7,8},{8,9},{9,10},{10,1... | collective-permute-start | bytes 786440 | tf_op jit(solution)/shard_map/ppermute | solution.py:21
  53.0 9.1 %copy-start.6 = (s32[1,1,1,512,256]{4,3,2,1,0:T(8,128)S(1)}, s32[1,1,1,512,256]{4,3,2,1,0:T(8,128)}, u32[]{:S(2)}) copy-start(s32[1,1,1,512,256]{4,3,2,1,0:T(8,128)} %get-tuple-element.10) | copy-start | bytes 1572868
  53.0 9.1 %copy-start.19 = (bf16[1,1,1,512,256]{4,3,2,1,0:T(8,128)(2,1)S(1)}, bf16[1,1,1,512,256]{4,3,2,1,0:T(8,128)(2,1)}, u32[]{:S(2)}) copy-start(bf16[1,1,1,512,256]{4,3,2,1,0:T(8,128)(2,1)} %get-tuple-element.18) | copy-start | bytes 786436
  64.6 12.0 %copy-start.5 = (s32[1,1,1,512,256]{4,3,2,1,0:T(8,128)S(1)}, s32[1,1,1,512,256]{4,3,2,1,0:T(8,128)}, u32[]{:S(2)}) copy-start(s32[1,1,1,512,256]{4,3,2,1,0:T(8,128)} %get-tuple-element.9) | copy-start | bytes 1572868
  64.6 12.0 %copy-start.18 = (bf16[1,1,1,512,256]{4,3,2,1,0:T(8,128)(2,1)S(1)}, bf16[1,1,1,512,256]{4,3,2,1,0:T(8,128)(2,1)}, u32[]{:S(2)}) copy-start(bf16[1,1,1,512,256]{4,3,2,1,0:T(8,128)(2,1)} %get-tuple-element.17) | copy-start | bytes 786436
  64.6 12.0 %collective-permute-start.6 = (f32[256,256]{1,0:T(8,128)S(1)}, f32[256,256]{1,0:T(8,128)S(1)}, u32[]{:S(2)}, u32[]{:S(2)}) collective-permute-start(f32[256,256]{1,0:T(8,128)S(1)} %fusion.32), channel_id=1, source_target_pairs={{0,1},{1,2},{2,3},{3,4},{4,5},{5,6},{6,7},{7,8},{8,9},{9,10},{10,1... | collective-permute-start | bytes 786440 | tf_op jit(solution)/shard_map/ppermute | solution.py:21
  79.1 12.2 %copy-start.4 = (s32[1,1,1,512,256]{4,3,2,1,0:T(8,128)S(1)}, s32[1,1,1,512,256]{4,3,2,1,0:T(8,128)}, u32[]{:S(2)}) copy-start(s32[1,1,1,512,256]{4,3,2,1,0:T(8,128)} %get-tuple-element.8) | copy-start | bytes 1572868
  79.1 12.2 %copy-start.17 = (bf16[1,1,1,512,256]{4,3,2,1,0:T(8,128)(2,1)S(1)}, bf16[1,1,1,512,256]{4,3,2,1,0:T(8,128)(2,1)}, u32[]{:S(2)}) copy-start(bf16[1,1,1,512,256]{4,3,2,1,0:T(8,128)(2,1)} %get-tuple-element.16) | copy-start | bytes 786436
  79.2 12.2 %collective-permute-start.7 = (f32[256,256]{1,0:T(8,128)S(1)}, f32[256,256]{1,0:T(8,128)S(1)}, u32[]{:S(2)}, u32[]{:S(2)}) collective-permute-start(f32[256,256]{1,0:T(8,128)S(1)} %fusion.28), channel_id=1, source_target_pairs={{0,1},{1,2},{2,3},{3,4},{4,5},{5,6},{6,7},{7,8},{8,9},{9,10},{10,1... | collective-permute-start | bytes 786440 | tf_op jit(solution)/shard_map/ppermute | solution.py:21
  93.9 11.4 %copy-start.3 = (s32[1,1,1,512,256]{4,3,2,1,0:T(8,128)S(1)}, s32[1,1,1,512,256]{4,3,2,1,0:T(8,128)}, u32[]{:S(2)}) copy-start(s32[1,1,1,512,256]{4,3,2,1,0:T(8,128)} %get-tuple-element.7) | copy-start | bytes 1572868
  93.9 11.4 %copy-start.16 = (bf16[1,1,1,512,256]{4,3,2,1,0:T(8,128)(2,1)S(1)}, bf16[1,1,1,512,256]{4,3,2,1,0:T(8,128)(2,1)}, u32[]{:S(2)}) copy-start(bf16[1,1,1,512,256]{4,3,2,1,0:T(8,128)(2,1)} %get-tuple-element.15) | copy-start | bytes 786436
  93.9 11.4 %collective-permute-start.8 = (f32[256,256]{1,0:T(8,128)S(1)}, f32[256,256]{1,0:T(8,128)S(1)}, u32[]{:S(2)}, u32[]{:S(2)}) collective-permute-start(f32[256,256]{1,0:T(8,128)S(1)} %fusion.24), channel_id=1, source_target_pairs={{0,1},{1,2},{2,3},{3,4},{4,5},{5,6},{6,7},{7,8},{8,9},{9,10},{10,1... | collective-permute-start | bytes 786440 | tf_op jit(solution)/shard_map/ppermute | solution.py:21
  107.8 10.8 %copy-start.15 = (bf16[1,1,1,512,256]{4,3,2,1,0:T(8,128)(2,1)S(1)}, bf16[1,1,1,512,256]{4,3,2,1,0:T(8,128)(2,1)}, u32[]{:S(2)}) copy-start(bf16[1,1,1,512,256]{4,3,2,1,0:T(8,128)(2,1)} %get-tuple-element.21) | copy-start | bytes 786436
  107.9 10.8 %collective-permute-start.9 = (f32[256,256]{1,0:T(8,128)S(1)}, f32[256,256]{1,0:T(8,128)S(1)}, u32[]{:S(2)}, u32[]{:S(2)}) collective-permute-start(f32[256,256]{1,0:T(8,128)S(1)} %fusion.20), channel_id=1, source_target_pairs={{0,1},{1,2},{2,3},{3,4},{4,5},{5,6},{6,7},{7,8},{8,9},{9,10},{10,1... | collective-permute-start | bytes 786440 | tf_op jit(solution)/shard_map/ppermute | solution.py:21
  121.1 9.8 %copy-start.14 = (bf16[1,1,1,512,256]{4,3,2,1,0:T(8,128)(2,1)S(1)}, bf16[1,1,1,512,256]{4,3,2,1,0:T(8,128)(2,1)}, u32[]{:S(2)}) copy-start(bf16[1,1,1,512,256]{4,3,2,1,0:T(8,128)(2,1)} %get-tuple-element.14) | copy-start | bytes 786436
  121.2 9.8 %collective-permute-start.10 = (f32[256,256]{1,0:T(8,128)S(1)}, f32[256,256]{1,0:T(8,128)S(1)}, u32[]{:S(2)}, u32[]{:S(2)}) collective-permute-start(f32[256,256]{1,0:T(8,128)S(1)} %fusion.16), channel_id=1, source_target_pairs={{0,1},{1,2},{2,3},{3,4},{4,5},{5,6},{6,7},{7,8},{8,9},{9,10},{10,1... | collective-permute-start | bytes 786440 | tf_op jit(solution)/shard_map/ppermute | solution.py:21
  (12 other events, 27.8 us)

commit v2 on v1

--- a/solution.py
+++ b/solution.py
@@ -44,7 +44,14 @@
     sub_count = user_rows // TILE
     half_span = lax.axis_size("users") // 2
     sources = ((-half_span, half_span), (2, -2), (1, -1), (-1, 1))
-    neighbours = [passed_along(own_block, "users", steps) for steps, _ in sources]
+    far_block = passed_along(own_block, "users", -half_span)
+    minus_two = passed_along(own_block, "users", 2)
+    plus_one = passed_along(own_block, "users", -1)
+    count = lax.axis_size("users")
+    odd = lax.axis_index("users") % 2 == 1
+    relay = jnp.where(odd, minus_two, own_block)
+    minus_one = lax.ppermute(relay, "users", [(s, s ^ 1) for s in range(count)])
+    neighbours = [far_block, minus_two, minus_one, plus_one]
     mixings = []
     for _, offset in sources:
         picked = (offsets == offset) & (jnp.arange(MAX_LINKS) < count_used)

time: 137 us -> 146 us (1.066)
  the two profiles are of different devices: /device:TPU:0 before, /device:TPU:128 now
where the time goes in v2:
time: 146 us
  waiting for transfers between devices  68.7 us (47%)
  matrix products  34.1 us (23%)
  between operations  22.3 us (15%)
  local copies, waits for them, and re-layouts  9.62 us (7%)
  starting transfers between devices  8.59 us (6%)
  other arithmetic  2.3 us (2%)
    ppermute x10, waiting for transfers between devices, passed_along(): return lax.ppermute(value, axis, pairs)  68.7 us
    dot_general x32, matrix products, chain_part(): lax.dot_general(residual_err, block_rows, (((0,), (0,)), ((), ())), preci...  11.4 us
    dot_general x32, matrix products, chain_part(): lax.dot_general(block_rows, part, (((1,), (1,)), ((), ())), precision=STEP)  10.7 us
    dot_general x32, matrix products, shards(): grad_users = grad_users + jnp.dot(errors[c][k], held[c][k], precision=STEP)  9.57 us
    ppermute x10, starting transfers between devices, passed_along(): return lax.ppermute(value, axis, pairs)  7.92 us
  transfers between devices with their start and end apart: 11, of which 7 were waited for; matrix products, arithmetic and copies ran while one was open for 17% of the time, Pallas kernels for 0%

profile of v2, /device:TPU:128, one launch (start us, length us, event | category | flops | bytes accessed | tf_op | source)
XLA Modules:
  0.0 145.6 jit_solution(6292115265173607847)
XLA Ops:
  0.7 1.4 collective-permute-start.1
  2.1 2.6 %collective-permute-start = (f32[512,256]{1,0:T(8,128)}, f32[512,256]{1,0:T(8,128)}, u32[]{:S(2)}, u32[]{:S(2)}) collective-permute-start(f32[512,256]{1,0:T(8,128)} %bitcast.459), channel_id=1, source_target_pairs={{0,128},{16,144},{32,160},{48,176},{64,192},{80,208},{96,224},{112... | collective-permute-start | bytes 1572872 | tf_op jit(solution)/shard_map/ppermute | solution.py:21
  4.7 1.8 %fusion.334 = (s32[1,1]{0,1:T(1,128)}, s32[1,1]{0,1:T(1,128)}, s32[1,1]{0,1:T(1,128)}, s32[1,1]{0,1:T(1,128)}, s32[1,1]{0,1:T(1,128)}, /*index=5*/s32[1,1]{0,1:T...) fusion(s32[8,4]{0,1:T(4,128)} %param.15), kind=kLoop, calls=%fused_computation.439 | loop fusion | bytes 104 | tf_op jit(solution)/shard_map/slice | solution.py:88
  9.0 2.9 %fusion.332 = (bf16[1,1,1,512,256]{4,3,2,1,0:T(8,128)(2,1)}, bf16[1,1,1,512,256]{4,3,2,1,0:T(8,128)(2,1)}, bf16[1,1,1,512,256]{4,3,2,1,0:T(8,128)(2,1)}, bf16[1,...) fusion(bf16[1,1,8,512,256]{4,3,2,1,0:T(8,128)(2,1)} %param.10), kind=kLoop, calls=%fused_computation.437 | loop fusion | bytes 4194304 | tf_op jit(solution)/shard_map/slice | solution.py:86
  12.3 1.5 %fusion.331 = (s32[1,1,1,512,256]{4,3,2,1,0:T(8,128)S(1)}, s32[1,1,1,512,256]{4,3,2,1,0:T(8,128)}, s32[1,1,1,512,256]{4,3,2,1,0:T(8,128)}, s32[1,1,1,512,256]{4,...) fusion(s32[1,1,8,512,256]{4,3,2,1,0:T(8,128)S(1)} %copy-done.1), kind=kLoop, calls=%fused_computation.436 | loop fusion | bytes 8388608 | tf_op jit(solution)/shard_map/slice | solution.py:87
  15.9 1.2 fusion.163
  17.1 1.0 fusion.40
  18.2 1.5 %collective-permute-start.4 = (f32[256,256]{1,0:T(8,128)}, f32[256,256]{1,0:T(8,128)S(1)}, u32[]{:S(2)}, u32[]{:S(2)}) collective-permute-start(f32[256,256]{1,0:T(8,128)} %fusion.40), channel_id=1, source_target_pairs={{0,1},{1,2},{2,3},{3,4},{4,5},{5,6},{6,7},{7,8},{8,9},{9,10},{10,1... | collective-permute-start | bytes 786440 | tf_op jit(solution)/shard_map/ppermute | solution.py:21
  20.3 1.3 fusion.183
  21.7 1.1 fusion.174
  22.9 1.2 fusion.170
  24.1 14.9 %collective-permute-done.1 = f32[512,256]{1,0:T(8,128)} collective-permute-done((f32[512,256]{1,0:T(8,128)}, f32[512,256]{1,0:T(8,128)}, u32[]{:S(2)}, u32[]{:S(2)}) %collective-permute-start.1) | collective-permute-done | bytes 524320 | tf_op jit(solution)/shard_map/ppermute | solution.py:21
  39.0 0.9 broadcast_select_fusion
  59.3 2.5 %fusion.187 = f32[4,128,256]{2,1,0:T(8,128)S(1)} fusion(f32[1,4,128,256]{3,2,0,1:T(8,128)} %bitcast.35, f32[1,4,128,256]{3,2,0,1:T(8,128)} %bitcast.33, f32[1,4,128,256]{3,2,0,1:T(8,128)} %bitcast.31, f32[1,4,128,256]{3,2,0,1:T(8,128)} %bitcast.29, f32[1,4,128,128]{3,2,0,1:T(8,128)} %bitcast.464, f32[1,4,128,128]{3,2,0,1:T(8,128)} %bitcast.463, ...), kind=kOutput, calls=%fused_computation.286 | convolution fusion | flops 405143552 | bytes 3670020 | tf_op jit(solution)/shard_map/bgcj,bgjz->gcz/dot_general | solution.py:62
  62.0 0.9 copy-done.7
  65.4 1.7 %collective-permute-start.5 = (f32[256,256]{1,0:T(8,128)S(1)}, f32[256,256]{1,0:T(8,128)S(1)}, u32[]{:S(2)}, u32[]{:S(2)}) collective-permute-start(f32[256,256]{1,0:T(8,128)S(1)} %fusion.36), channel_id=1, source_target_pairs={{0,1},{1,2},{2,3},{3,4},{4,5},{5,6},{6,7},{7,8},{8,9},{9,10},{10,1... | collective-permute-start | bytes 786440 | tf_op jit(solution)/shard_map/ppermute | solution.py:21
  68.2 9.2 %collective-permute-done.5 = f32[256,256]{1,0:T(8,128)S(1)} collective-permute-done((f32[256,256]{1,0:T(8,128)S(1)}, f32[256,256]{1,0:T(8,128)S(1)}, u32[]{:S(2)}, u32[]{:S(2)}) %collective-permute-start.5) | collective-permute-done | bytes 262176 | tf_op jit(solution)/shard_map/ppermute | solution.py:21
  81.1 9.8 %collective-permute-done.6 = f32[256,256]{1,0:T(8,128)S(1)} collective-permute-done((f32[256,256]{1,0:T(8,128)S(1)}, f32[256,256]{1,0:T(8,128)S(1)}, u32[]{:S(2)}, u32[]{:S(2)}) %collective-permute-start.6) | collective-permute-done | bytes 262176 | tf_op jit(solution)/shard_map/ppermute | solution.py:21
  94.6 8.9 %collective-permute-done.7 = f32[256,256]{1,0:T(8,128)S(1)} collective-permute-done((f32[256,256]{1,0:T(8,128)S(1)}, f32[256,256]{1,0:T(8,128)S(1)}, u32[]{:S(2)}, u32[]{:S(2)}) %collective-permute-start.7) | collective-permute-done | bytes 262176 | tf_op jit(solution)/shard_map/ppermute | solution.py:21
  107.1 8.6 %collective-permute-done.8 = f32[256,256]{1,0:T(8,128)S(1)} collective-permute-done((f32[256,256]{1,0:T(8,128)S(1)}, f32[256,256]{1,0:T(8,128)S(1)}, u32[]{:S(2)}, u32[]{:S(2)}) %collective-permute-start.8) | collective-permute-done | bytes 262176 | tf_op jit(solution)/shard_map/ppermute | solution.py:21
  119.6 8.6 %collective-permute-done.9 = f32[256,256]{1,0:T(8,128)S(1)} collective-permute-done((f32[256,256]{1,0:T(8,128)S(1)}, f32[256,256]{1,0:T(8,128)S(1)}, u32[]{:S(2)}, u32[]{:S(2)}) %collective-permute-start.9) | collective-permute-done | bytes 262176 | tf_op jit(solution)/shard_map/ppermute | solution.py:21
  132.0 8.6 %collective-permute-done.10 = f32[256,256]{1,0:T(8,128)S(1)} collective-permute-done((f32[256,256]{1,0:T(8,128)S(1)}, f32[256,256]{1,0:T(8,128)S(1)}, u32[]{:S(2)}, u32[]{:S(2)}) %collective-permute-start.10) | collective-permute-done | bytes 262176 | tf_op jit(solution)/shard_map/ppermute | solution.py:21
  142.8 1.0 fusion.12
  144.8 0.8 copy-done.21
  (161 shorter events, 29.1 us)
Async XLA Ops:
  0.6 58.6 %collective-permute-start.3 = (f32[512,256]{1,0:T(8,128)}, f32[512,256]{1,0:T(8,128)}, u32[]{:S(2)}, u32[]{:S(2)}) collective-permute-start(f32[512,256]{1,0:T(8,128)} %bitcast.457), channel_id=1, source_target_pairs={{0,240},{16,0},{32,16},{48,32},{64,48},{80,64},{96,80},{112,96},{1... | collective-permute-start | bytes 1572872 | tf_op jit(solution)/shard_map/ppermute | solution.py:21
  0.7 38.3 %collective-permute-start.1 = (f32[512,256]{1,0:T(8,128)}, f32[512,256]{1,0:T(8,128)}, u32[]{:S(2)}, u32[]{:S(2)}) collective-permute-start(f32[512,256]{1,0:T(8,128)} %bitcast.458), channel_id=1, source_target_pairs={{0,32},{16,48},{32,64},{48,80},{64,96},{80,112},{96,128},{112,144}... | collective-permute-start | bytes 1572872 | tf_op jit(solution)/shard_map/ppermute | solution.py:21
  2.1 57.2 %collective-permute-start = (f32[512,256]{1,0:T(8,128)}, f32[512,256]{1,0:T(8,128)}, u32[]{:S(2)}, u32[]{:S(2)}) collective-permute-start(f32[512,256]{1,0:T(8,128)} %bitcast.459), channel_id=1, source_target_pairs={{0,128},{16,144},{32,160},{48,176},{64,192},{80,208},{96,224},{112... | collective-permute-start | bytes 1572872 | tf_op jit(solution)/shard_map/ppermute | solution.py:21
  18.2 43.8 %collective-permute-start.4 = (f32[256,256]{1,0:T(8,128)}, f32[256,256]{1,0:T(8,128)S(1)}, u32[]{:S(2)}, u32[]{:S(2)}) collective-permute-start(f32[256,256]{1,0:T(8,128)} %fusion.40), channel_id=1, source_target_pairs={{0,1},{1,2},{2,3},{3,4},{4,5},{5,6},{6,7},{7,8},{8,9},{9,10},{10,1... | collective-permute-start | bytes 786440 | tf_op jit(solution)/shard_map/ppermute | solution.py:21
  21.7 18.9 %copy-start.23 = (s32[8,4]{0,1:T(4,128)S(1)}, s32[8,4]{0,1:T(4,128)}, u32[]{:S(2)}) copy-start(s32[8,4]{0,1:T(4,128)} %param.15) | copy-start | bytes 388
  22.9 36.1 %copy-start.9 = (f32[128,256]{1,0:T(8,128)S(1)}, f32[128,256]{1,0:T(8,128)}, u32[]{:S(2)}) copy-start(f32[128,256]{1,0:T(8,128)} %copy-done.8) | copy-start | bytes 393220
  24.1 35.2 %copy-start.22 = (f32[4,128,128]{2,1,0:T(8,128)S(1)}, f32[4,128,128]{2,1,0:T(8,128)}, u32[]{:S(2)}) copy-start(f32[4,128,128]{2,1,0:T(8,128)} %get-tuple-element.2) | copy-start | bytes 786436
  39.9 19.4 %collective-permute-start.2 = (f32[512,256]{1,0:T(8,128)}, f32[512,256]{1,0:T(8,128)}, u32[]{:S(2)}, u32[]{:S(2)}) collective-permute-start(f32[512,256]{1,0:T(8,128)} %broadcast_select_fusion), channel_id=1, source_target_pairs={{0,16},{16,0},{32,48},{48,32},{64,80},{80,64},{96,112},{112,96},{1... | collective-permute-start | bytes 1572872 | tf_op jit(solution)/shard_map/ppermute | solution.py:53
  65.4 11.9 %collective-permute-start.5 = (f32[256,256]{1,0:T(8,128)S(1)}, f32[256,256]{1,0:T(8,128)S(1)}, u32[]{:S(2)}, u32[]{:S(2)}) collective-permute-start(f32[256,256]{1,0:T(8,128)S(1)} %fusion.36), channel_id=1, source_target_pairs={{0,1},{1,2},{2,3},{3,4},{4,5},{5,6},{6,7},{7,8},{8,9},{9,10},{10,1... | collective-permute-start | bytes 786440 | tf_op jit(solution)/shard_map/ppermute | solution.py:21
  67.2 10.2 %copy-start.6 = (s32[1,1,1,512,256]{4,3,2,1,0:T(8,128)S(1)}, s32[1,1,1,512,256]{4,3,2,1,0:T(8,128)}, u32[]{:S(2)}) copy-start(s32[1,1,1,512,256]{4,3,2,1,0:T(8,128)} %get-tuple-element.10) | copy-start | bytes 1572868
  67.2 10.2 %copy-start.18 = (bf16[1,1,1,512,256]{4,3,2,1,0:T(8,128)(2,1)S(1)}, bf16[1,1,1,512,256]{4,3,2,1,0:T(8,128)(2,1)}, u32[]{:S(2)}) copy-start(bf16[1,1,1,512,256]{4,3,2,1,0:T(8,128)(2,1)} %get-tuple-element.18) | copy-start | bytes 786436
  79.9 11.0 %copy-start.5 = (s32[1,1,1,512,256]{4,3,2,1,0:T(8,128)S(1)}, s32[1,1,1,512,256]{4,3,2,1,0:T(8,128)}, u32[]{:S(2)}) copy-start(s32[1,1,1,512,256]{4,3,2,1,0:T(8,128)} %get-tuple-element.9) | copy-start | bytes 1572868
  79.9 10.9 %copy-start.17 = (bf16[1,1,1,512,256]{4,3,2,1,0:T(8,128)(2,1)S(1)}, bf16[1,1,1,512,256]{4,3,2,1,0:T(8,128)(2,1)}, u32[]{:S(2)}) copy-start(bf16[1,1,1,512,256]{4,3,2,1,0:T(8,128)(2,1)} %get-tuple-element.17) | copy-start | bytes 786436
  79.9 10.9 %collective-permute-start.6 = (f32[256,256]{1,0:T(8,128)S(1)}, f32[256,256]{1,0:T(8,128)S(1)}, u32[]{:S(2)}, u32[]{:S(2)}) collective-permute-start(f32[256,256]{1,0:T(8,128)S(1)} %fusion.32), channel_id=1, source_target_pairs={{0,1},{1,2},{2,3},{3,4},{4,5},{5,6},{6,7},{7,8},{8,9},{9,10},{10,1... | collective-permute-start | bytes 786440 | tf_op jit(solution)/shard_map/ppermute | solution.py:21
  93.4 10.0 %copy-start.4 = (s32[1,1,1,512,256]{4,3,2,1,0:T(8,128)S(1)}, s32[1,1,1,512,256]{4,3,2,1,0:T(8,128)}, u32[]{:S(2)}) copy-start(s32[1,1,1,512,256]{4,3,2,1,0:T(8,128)} %get-tuple-element.8) | copy-start | bytes 1572868
  93.4 10.0 %copy-start.16 = (bf16[1,1,1,512,256]{4,3,2,1,0:T(8,128)(2,1)S(1)}, bf16[1,1,1,512,256]{4,3,2,1,0:T(8,128)(2,1)}, u32[]{:S(2)}) copy-start(bf16[1,1,1,512,256]{4,3,2,1,0:T(8,128)(2,1)} %get-tuple-element.16) | copy-start | bytes 786436
  93.4 10.0 %collective-permute-start.7 = (f32[256,256]{1,0:T(8,128)S(1)}, f32[256,256]{1,0:T(8,128)S(1)}, u32[]{:S(2)}, u32[]{:S(2)}) collective-permute-start(f32[256,256]{1,0:T(8,128)S(1)} %fusion.28), channel_id=1, source_target_pairs={{0,1},{1,2},{2,3},{3,4},{4,5},{5,6},{6,7},{7,8},{8,9},{9,10},{10,1... | collective-permute-start | bytes 786440 | tf_op jit(solution)/shard_map/ppermute | solution.py:21
  106.0 9.8 %copy-start.3 = (s32[1,1,1,512,256]{4,3,2,1,0:T(8,128)S(1)}, s32[1,1,1,512,256]{4,3,2,1,0:T(8,128)}, u32[]{:S(2)}) copy-start(s32[1,1,1,512,256]{4,3,2,1,0:T(8,128)} %get-tuple-element.7) | copy-start | bytes 1572868
  106.0 9.8 %copy-start.15 = (bf16[1,1,1,512,256]{4,3,2,1,0:T(8,128)(2,1)S(1)}, bf16[1,1,1,512,256]{4,3,2,1,0:T(8,128)(2,1)}, u32[]{:S(2)}) copy-start(bf16[1,1,1,512,256]{4,3,2,1,0:T(8,128)(2,1)} %get-tuple-element.15) | copy-start | bytes 786436
  106.0 9.8 %collective-permute-start.8 = (f32[256,256]{1,0:T(8,128)S(1)}, f32[256,256]{1,0:T(8,128)S(1)}, u32[]{:S(2)}, u32[]{:S(2)}) collective-permute-start(f32[256,256]{1,0:T(8,128)S(1)} %fusion.24), channel_id=1, source_target_pairs={{0,1},{1,2},{2,3},{3,4},{4,5},{5,6},{6,7},{7,8},{8,9},{9,10},{10,1... | collective-permute-start | bytes 786440 | tf_op jit(solution)/shard_map/ppermute | solution.py:21
  118.3 10.0 %copy-start.14 = (bf16[1,1,1,512,256]{4,3,2,1,0:T(8,128)(2,1)S(1)}, bf16[1,1,1,512,256]{4,3,2,1,0:T(8,128)(2,1)}, u32[]{:S(2)}) copy-start(bf16[1,1,1,512,256]{4,3,2,1,0:T(8,128)(2,1)} %get-tuple-element.21) | copy-start | bytes 786436
  118.3 10.0 %collective-permute-start.9 = (f32[256,256]{1,0:T(8,128)S(1)}, f32[256,256]{1,0:T(8,128)S(1)}, u32[]{:S(2)}, u32[]{:S(2)}) collective-permute-start(f32[256,256]{1,0:T(8,128)S(1)} %fusion.20), channel_id=1, source_target_pairs={{0,1},{1,2},{2,3},{3,4},{4,5},{5,6},{6,7},{7,8},{8,9},{9,10},{10,1... | collective-permute-start | bytes 786440 | tf_op jit(solution)/shard_map/ppermute | solution.py:21
  130.8 9.8 %copy-start.13 = (bf16[1,1,1,512,256]{4,3,2,1,0:T(8,128)(2,1)S(1)}, bf16[1,1,1,512,256]{4,3,2,1,0:T(8,128)(2,1)}, u32[]{:S(2)}) copy-start(bf16[1,1,1,512,256]{4,3,2,1,0:T(8,128)(2,1)} %get-tuple-element.14) | copy-start | bytes 786436
  130.8 9.8 %collective-permute-start.10 = (f32[256,256]{1,0:T(8,128)S(1)}, f32[256,256]{1,0:T(8,128)S(1)}, u32[]{:S(2)}, u32[]{:S(2)}) collective-permute-start(f32[256,256]{1,0:T(8,128)S(1)} %fusion.16), channel_id=1, source_target_pairs={{0,1},{1,2},{2,3},{3,4},{4,5},{5,6},{6,7},{7,8},{8,9},{9,10},{10,1... | collective-permute-start | bytes 786440 | tf_op jit(solution)/shard_map/ppermute | solution.py:21
  (12 other events, 35.5 us)

commit v3 on v1

--- a/solution.py
+++ b/solution.py
@@ -44,7 +44,12 @@
     sub_count = user_rows // TILE
     half_span = lax.axis_size("users") // 2
     sources = ((-half_span, half_span), (2, -2), (1, -1), (-1, 1))
-    neighbours = [passed_along(own_block, "users", steps) for steps, _ in sources]
+    quarter = half_span // 2
+    split = (5 * user_rows) // 8
+    one_way = passed_along(passed_along(own_block[:split], "users", -quarter), "users", -quarter)
+    other_way = passed_along(passed_along(own_block[split:], "users", quarter), "users", quarter)
+    far_block = jnp.concatenate([one_way, other_way], axis=0)
+    neighbours = [far_block] + [passed_along(own_block, "users", steps) for steps, _ in sources[1:]]
     mixings = []
     for _, offset in sources:
         picked = (offsets == offset) & (jnp.arange(MAX_LINKS) < count_used)

time: 137 us -> 157 us (1.15)
  waiting for transfers between devices: 58.1 us -> 72.7 us
  local copies, waits for them, and re-layouts: 9.63 us -> 12.6 us
  starting transfers between devices: 10.9 us -> 13.2 us
    ppermute x11 -> x14, waiting for transfers between devices: 58.1 us -> 72.7 us  [passed_along(): return lax.ppermute(value, axis, pairs)]
    slice x0 -> x2, local copies, waits for them, and re-layouts: none -> 3.4 us  [the longest x1 1.72 us: graph_target(): own_block[:split]]
    dot_general x32, matrix products: 10.7 us -> 13.4 us  [chain_part(): lax.dot_general(block_rows, part, (((1,), (1,)), ((), ())), precision=STEP)]
    ppermute x11 -> x14, starting transfers between devices: 10.9 us -> 13.2 us  [passed_along(): return lax.ppermute(value, axis, pairs)]
    unnamed x58 -> x44, local copies, waits for them, and re-layouts: 2.63 us -> 3.76 us
  transfers between devices with their start and end apart: 11 -> 14, of which waited for: 6 -> 9; matrix products, arithmetic and copies ran while one was open for 17% -> 17% of each run, Pallas kernels for 0% -> 0%
where the time goes in v3:
time: 157 us
  waiting for transfers between devices  72.7 us (46%)
  matrix products  33.9 us (22%)
  between operations  22.4 us (14%)
  starting transfers between devices  13.2 us (8%)
  local copies, waits for them, and re-layouts  12.6 us (8%)
  other arithmetic  1.85 us (1%)
    ppermute x14, waiting for transfers between devices, passed_along(): return lax.ppermute(value, axis, pairs)  72.7 us
    dot_general x32, matrix products, chain_part(): lax.dot_general(block_rows, part, (((1,), (1,)), ((), ())), precision=STEP)  13.4 us
    ppermute x14, starting transfers between devices, passed_along(): return lax.ppermute(value, axis, pairs)  13.2 us
    dot_general x32, matrix products, chain_part(): lax.dot_general(residual_err, block_rows, (((0,), (0,)), ((), ())), preci...  10.6 us
    dot_general x32, matrix products, shards(): grad_users = grad_users + jnp.dot(errors[c][k], held[c][k], precision=STEP)  7.74 us
    unnamed x44, local copies, waits for them, and re-layouts  3.76 us
  transfers between devices with their start and end apart: 14, of which 9 were waited for; matrix products, arithmetic and copies ran while one was open for 17% of the time, Pallas kernels for 0%

profile of v3, /device:TPU:0, one launch (start us, length us, event | category | flops | bytes accessed | tf_op | source)
XLA Modules:
  0.0 156.7 jit_solution(3095280905007092422)
XLA Ops:
  0.6 3.6 %collective-permute-start.6 = (f32[512,256]{1,0:T(8,128)}, f32[512,256]{1,0:T(8,128)}, u32[]{:S(2)}, u32[]{:S(2)}) collective-permute-start(f32[512,256]{1,0:T(8,128)} %bitcast.458), channel_id=1, source_target_pairs={{0,240},{16,0},{32,16},{48,32},{64,48},{80,64},{96,80},{112,96},{1... | collective-permute-start | bytes 1572872 | tf_op jit(solution)/shard_map/ppermute | solution.py:21
  4.2 1.7 %slice_bitcast_fusion.1 = f32[192,256]{1,0:T(8,128)} fusion(f32[1,1,512,256]{3,2,1,0:T(8,128)} %param.8), kind=kLoop, calls=%fused_computation.291 | loop fusion | bytes 393216 | tf_op jit(solution)/shard_map/slice | solution.py:50
  6.3 1.7 %slice_bitcast_fusion = f32[320,256]{1,0:T(8,128)} fusion(f32[1,1,512,256]{3,2,1,0:T(8,128)} %param.8), kind=kLoop, calls=%fused_computation.288 | loop fusion | bytes 655360 | tf_op jit(solution)/shard_map/slice | solution.py:49
  8.0 3.8 %collective-permute-start = (f32[320,256]{1,0:T(8,128)}, f32[320,256]{1,0:T(8,128)}, u32[]{:S(2)}, u32[]{:S(2)}) collective-permute-start(f32[320,256]{1,0:T(8,128)} %slice_bitcast_fusion), channel_id=1, source_target_pairs={{0,192},{16,208},{32,224},{48,240},{64,0},{80,16},{96,32},{112,48}... | collective-permute-start | bytes 983048 | tf_op jit(solution)/shard_map/ppermute | solution.py:21
  11.8 1.8 %fusion.334 = (s32[1,1]{0,1:T(1,128)}, s32[1,1]{0,1:T(1,128)}, s32[1,1]{0,1:T(1,128)}, s32[1,1]{0,1:T(1,128)}, s32[1,1]{0,1:T(1,128)}, /*index=5*/s32[1,1]{0,1:T...) fusion(s32[8,4]{0,1:T(4,128)} %param.15), kind=kLoop, calls=%fused_computation.441 | loop fusion | bytes 104 | tf_op jit(solution)/shard_map/slice | solution.py:86
  22.8 1.4 fusion.332
  24.1 1.6 %copy-done.1 = s32[1,1,8,512,256]{4,3,2,1,0:T(8,128)S(1)} copy-done((s32[1,1,8,512,256]{4,3,2,1,0:T(8,128)S(1)}, s32[1,1,8,512,256]{4,3,2,1,0:T(8,128)}, u32[]{:S(2)}) %copy-start.1) | copy-done | bytes 4194328
  25.7 1.5 fusion.331
  29.1 1.2 fusion.171
  30.9 1.2 fusion.167
  47.7 1.4 collective-permute-start.1
  49.1 1.7 %collective-permute-start.3 = (f32[192,256]{1,0:T(8,128)}, f32[192,256]{1,0:T(8,128)S(1)}, u32[]{:S(2)}, u32[]{:S(2)}) collective-permute-start(f32[192,256]{1,0:T(8,128)} %collective-permute-done.2), channel_id=1, source_target_pairs={{0,64},{16,80},{32,96},{48,112},{64,128},{80,144},{96,160},{112,17... | collective-permute-start | bytes 589832 | tf_op jit(solution)/shard_map/ppermute | solution.py:21
  50.8 1.7 %fusion.183 = (f32[4,128,128]{2,1,0:T(8,128)S(1)}, f32[4,128,128]{2,1,0:T(8,128)S(1)}, f32[4,128,128]{2,1,0:T(8,128)S(1)}, f32[4,128,128]{2,1,0:T(8,128)S(1)}) fusion(f32[1,1,4,4,128,128]{5,4,3,2,1,0:T(8,128)} %param.14, pred[4]{0:T(512)(128)(4,1)S(1)} %get-tuple-element.56, pred[4]{0:T(512)(128)(4,1)S(1)} %get-tuple-element.55, ...), kind=kLoop, calls=%fused_computation.281 | loop fusion | flops 1835008 | bytes 2097168 | tf_op jit(solution)/shard_map/reduce_sum | solution.py:57
  52.6 8.0 %collective-permute-done.3 = f32[192,256]{1,0:T(8,128)S(1)} collective-permute-done((f32[192,256]{1,0:T(8,128)}, f32[192,256]{1,0:T(8,128)S(1)}, u32[]{:S(2)}, u32[]{:S(2)}) %collective-permute-start.3) | collective-permute-done | bytes 196640 | tf_op jit(solution)/shard_map/ppermute | solution.py:21
  60.6 1.5 collective-permute-start.7
  62.1 3.5 %collective-permute-done.1 = f32[320,256]{1,0:T(8,128)S(1)} collective-permute-done((f32[320,256]{1,0:T(8,128)}, f32[320,256]{1,0:T(8,128)S(1)}, u32[]{:S(2)}, u32[]{:S(2)}) %collective-permute-start.1) | collective-permute-done | bytes 327712 | tf_op jit(solution)/shard_map/ppermute | solution.py:21
  65.6 2.2 %fusion.187 = f32[4,128,256]{2,1,0:T(8,128)S(1)} fusion(f32[1,4,128,256]{3,2,0,1:T(8,128)} %bitcast.36, f32[1,4,128,256]{3,2,0,1:T(8,128)} %bitcast.34, f32[1,4,128,256]{3,2,0,1:T(8,128)} %bitcast.32, f32[1,4,128,256]{3,2,0,1:T(8,128)S(1)} %bitcast.462, f32[1,4,128,128]{3,2,0,1:T(8,128)S(1)} %bitcast.466, f32[1,4,128,128]{3,2,0,1:T(8,128)S(1)} %bitcast.465, ...), kind=kOutput, calls=%fused_computation.287 | convolution fusion | flops 405143552 | bytes 3670020 | tf_op jit(solution)/shard_map/bgcj,bgjz->gcz/dot_general | solution.py:60
  67.9 3.6 %collective-permute-done.7 = f32[256,256]{1,0:T(8,128)S(1)} collective-permute-done((f32[256,256]{1,0:T(8,128)S(1)}, f32[256,256]{1,0:T(8,128)S(1)}, u32[]{:S(2)}, u32[]{:S(2)}) %collective-permute-start.7) | collective-permute-done | bytes 262176 | tf_op jit(solution)/shard_map/ppermute | solution.py:21
  75.4 11.2 %collective-permute-done.8 = f32[256,256]{1,0:T(8,128)S(1)} collective-permute-done((f32[256,256]{1,0:T(8,128)S(1)}, f32[256,256]{1,0:T(8,128)S(1)}, u32[]{:S(2)}, u32[]{:S(2)}) %collective-permute-start.8) | collective-permute-done | bytes 262176 | tf_op jit(solution)/shard_map/ppermute | solution.py:21
  90.3 10.6 %collective-permute-done.9 = f32[256,256]{1,0:T(8,128)S(1)} collective-permute-done((f32[256,256]{1,0:T(8,128)S(1)}, f32[256,256]{1,0:T(8,128)S(1)}, u32[]{:S(2)}, u32[]{:S(2)}) %collective-permute-start.9) | collective-permute-done | bytes 262176 | tf_op jit(solution)/shard_map/ppermute | solution.py:21
  104.6 9.8 %collective-permute-done.10 = f32[256,256]{1,0:T(8,128)S(1)} collective-permute-done((f32[256,256]{1,0:T(8,128)S(1)}, f32[256,256]{1,0:T(8,128)S(1)}, u32[]{:S(2)}, u32[]{:S(2)}) %collective-permute-start.10) | collective-permute-done | bytes 262176 | tf_op jit(solution)/shard_map/ppermute | solution.py:21
  118.0 8.8 %collective-permute-done.11 = f32[256,256]{1,0:T(8,128)S(1)} collective-permute-done((f32[256,256]{1,0:T(8,128)S(1)}, f32[256,256]{1,0:T(8,128)S(1)}, u32[]{:S(2)}, u32[]{:S(2)}) %collective-permute-start.11) | collective-permute-done | bytes 262176 | tf_op jit(solution)/shard_map/ppermute | solution.py:21
  130.7 8.6 %collective-permute-done.12 = f32[256,256]{1,0:T(8,128)S(1)} collective-permute-done((f32[256,256]{1,0:T(8,128)S(1)}, f32[256,256]{1,0:T(8,128)S(1)}, u32[]{:S(2)}, u32[]{:S(2)}) %collective-permute-start.12) | collective-permute-done | bytes 262176 | tf_op jit(solution)/shard_map/ppermute | solution.py:21
  143.0 8.6 %collective-permute-done.13 = f32[256,256]{1,0:T(8,128)S(1)} collective-permute-done((f32[256,256]{1,0:T(8,128)S(1)}, f32[256,256]{1,0:T(8,128)S(1)}, u32[]{:S(2)}, u32[]{:S(2)}) %collective-permute-start.13) | collective-permute-done | bytes 262176 | tf_op jit(solution)/shard_map/ppermute | solution.py:21
  (155 shorter events, 33.6 us)
Async XLA Ops:
  0.6 22.1 %copy-start.3 = (bf16[1,1,8,512,256]{4,3,2,1,0:T(8,128)(2,1)S(1)}, bf16[1,1,8,512,256]{4,3,2,1,0:T(8,128)(2,1)}, u32[]{:S(2)}) copy-start(bf16[1,1,8,512,256]{4,3,2,1,0:T(8,128)(2,1)} %param.10) | copy-start | bytes 6291460
  0.6 65.0 %collective-permute-start.6 = (f32[512,256]{1,0:T(8,128)}, f32[512,256]{1,0:T(8,128)}, u32[]{:S(2)}, u32[]{:S(2)}) collective-permute-start(f32[512,256]{1,0:T(8,128)} %bitcast.458), channel_id=1, source_target_pairs={{0,240},{16,0},{32,16},{48,32},{64,48},{80,64},{96,80},{112,96},{1... | collective-permute-start | bytes 1572872 | tf_op jit(solution)/shard_map/ppermute | solution.py:21
  4.2 61.4 %collective-permute-start.5 = (f32[512,256]{1,0:T(8,128)}, f32[512,256]{1,0:T(8,128)}, u32[]{:S(2)}, u32[]{:S(2)}) collective-permute-start(f32[512,256]{1,0:T(8,128)} %bitcast.459), channel_id=1, source_target_pairs={{0,16},{16,32},{32,48},{48,64},{64,80},{80,96},{96,112},{112,128},... | collective-permute-start | bytes 1572872 | tf_op jit(solution)/shard_map/ppermute | solution.py:21
  4.2 61.4 %collective-permute-start.4 = (f32[512,256]{1,0:T(8,128)}, f32[512,256]{1,0:T(8,128)}, u32[]{:S(2)}, u32[]{:S(2)}) collective-permute-start(f32[512,256]{1,0:T(8,128)} %bitcast.460), channel_id=1, source_target_pairs={{0,32},{16,48},{32,64},{48,80},{64,96},{80,112},{96,128},{112,144}... | collective-permute-start | bytes 1572872 | tf_op jit(solution)/shard_map/ppermute | solution.py:21
  5.9 43.2 %collective-permute-start.2 = (f32[192,256]{1,0:T(8,128)}, f32[192,256]{1,0:T(8,128)}, u32[]{:S(2)}, u32[]{:S(2)}) collective-permute-start(f32[192,256]{1,0:T(8,128)} %slice_bitcast_fusion.1), channel_id=1, source_target_pairs={{0,64},{16,80},{32,96},{48,112},{64,128},{80,144},{96,160},{112,17... | collective-permute-start | bytes 589832 | tf_op jit(solution)/shard_map/ppermute | solution.py:21
  8.0 39.7 %collective-permute-start = (f32[320,256]{1,0:T(8,128)}, f32[320,256]{1,0:T(8,128)}, u32[]{:S(2)}, u32[]{:S(2)}) collective-permute-start(f32[320,256]{1,0:T(8,128)} %slice_bitcast_fusion), channel_id=1, source_target_pairs={{0,192},{16,208},{32,224},{48,240},{64,0},{80,16},{96,32},{112,48}... | collective-permute-start | bytes 983048 | tf_op jit(solution)/shard_map/ppermute | solution.py:21
  32.1 17.0 %copy-start.17 = (s32[1,1,4]{2,1,0:T(1,128)S(1)}, s32[1,1,4]{2,1,0:T(1,128)}, u32[]{:S(2)}) copy-start(s32[1,1,4]{2,1,0:T(1,128)} %param.12) | copy-start | bytes 52
  47.7 17.8 %collective-permute-start.1 = (f32[320,256]{1,0:T(8,128)}, f32[320,256]{1,0:T(8,128)S(1)}, u32[]{:S(2)}, u32[]{:S(2)}) collective-permute-start(f32[320,256]{1,0:T(8,128)} %collective-permute-done), channel_id=1, source_target_pairs={{0,192},{16,208},{32,224},{48,240},{64,0},{80,16},{96,32},{112,48}... | collective-permute-start | bytes 983048 | tf_op jit(solution)/shard_map/ppermute | solution.py:21
  49.1 11.5 %collective-permute-start.3 = (f32[192,256]{1,0:T(8,128)}, f32[192,256]{1,0:T(8,128)S(1)}, u32[]{:S(2)}, u32[]{:S(2)}) collective-permute-start(f32[192,256]{1,0:T(8,128)} %collective-permute-done.2), channel_id=1, source_target_pairs={{0,64},{16,80},{32,96},{48,112},{64,128},{80,144},{96,160},{112,17... | collective-permute-start | bytes 589832 | tf_op jit(solution)/shard_map/ppermute | solution.py:21
  60.6 11.0 %collective-permute-start.7 = (f32[256,256]{1,0:T(8,128)S(1)}, f32[256,256]{1,0:T(8,128)S(1)}, u32[]{:S(2)}, u32[]{:S(2)}) collective-permute-start(f32[256,256]{1,0:T(8,128)S(1)} %fusion.40), channel_id=1, source_target_pairs={{0,1},{1,2},{2,3},{3,4},{4,5},{5,6},{6,7},{7,8},{8,9},{9,10},{10,1... | collective-permute-start | bytes 786440 | tf_op jit(solution)/shard_map/ppermute | solution.py:21
  74.1 12.5 %collective-permute-start.8 = (f32[256,256]{1,0:T(8,128)S(1)}, f32[256,256]{1,0:T(8,128)S(1)}, u32[]{:S(2)}, u32[]{:S(2)}) collective-permute-start(f32[256,256]{1,0:T(8,128)S(1)} %fusion.36), channel_id=1, source_target_pairs={{0,1},{1,2},{2,3},{3,4},{4,5},{5,6},{6,7},{7,8},{8,9},{9,10},{10,1... | collective-permute-start | bytes 786440 | tf_op jit(solution)/shard_map/ppermute | solution.py:21
  74.4 12.2 %copy-start.6 = (s32[1,1,1,512,256]{4,3,2,1,0:T(8,128)S(1)}, s32[1,1,1,512,256]{4,3,2,1,0:T(8,128)}, u32[]{:S(2)}) copy-start(s32[1,1,1,512,256]{4,3,2,1,0:T(8,128)} %get-tuple-element.10) | copy-start | bytes 1572868
  74.4 12.2 %copy-start.13 = (bf16[1,1,1,512,256]{4,3,2,1,0:T(8,128)(2,1)S(1)}, bf16[1,1,1,512,256]{4,3,2,1,0:T(8,128)(2,1)}, u32[]{:S(2)}) copy-start(bf16[1,1,1,512,256]{4,3,2,1,0:T(8,128)(2,1)} %get-tuple-element.18) | copy-start | bytes 786436
  89.1 11.7 %copy-start.5 = (s32[1,1,1,512,256]{4,3,2,1,0:T(8,128)S(1)}, s32[1,1,1,512,256]{4,3,2,1,0:T(8,128)}, u32[]{:S(2)}) copy-start(s32[1,1,1,512,256]{4,3,2,1,0:T(8,128)} %get-tuple-element.9) | copy-start | bytes 1572868
  89.1 11.7 %copy-start.12 = (bf16[1,1,1,512,256]{4,3,2,1,0:T(8,128)(2,1)S(1)}, bf16[1,1,1,512,256]{4,3,2,1,0:T(8,128)(2,1)}, u32[]{:S(2)}) copy-start(bf16[1,1,1,512,256]{4,3,2,1,0:T(8,128)(2,1)} %get-tuple-element.17) | copy-start | bytes 786436
  89.2 11.7 %collective-permute-start.9 = (f32[256,256]{1,0:T(8,128)S(1)}, f32[256,256]{1,0:T(8,128)S(1)}, u32[]{:S(2)}, u32[]{:S(2)}) collective-permute-start(f32[256,256]{1,0:T(8,128)S(1)} %fusion.32), channel_id=1, source_target_pairs={{0,1},{1,2},{2,3},{3,4},{4,5},{5,6},{6,7},{7,8},{8,9},{9,10},{10,1... | collective-permute-start | bytes 786440 | tf_op jit(solution)/shard_map/ppermute | solution.py:21
  103.4 10.9 %copy-start.4 = (s32[1,1,1,512,256]{4,3,2,1,0:T(8,128)S(1)}, s32[1,1,1,512,256]{4,3,2,1,0:T(8,128)}, u32[]{:S(2)}) copy-start(s32[1,1,1,512,256]{4,3,2,1,0:T(8,128)} %get-tuple-element.8) | copy-start | bytes 1572868
  103.4 10.9 %copy-start.11 = (bf16[1,1,1,512,256]{4,3,2,1,0:T(8,128)(2,1)S(1)}, bf16[1,1,1,512,256]{4,3,2,1,0:T(8,128)(2,1)}, u32[]{:S(2)}) copy-start(bf16[1,1,1,512,256]{4,3,2,1,0:T(8,128)(2,1)} %get-tuple-element.16) | copy-start | bytes 786436
  103.4 10.9 %collective-permute-start.10 = (f32[256,256]{1,0:T(8,128)S(1)}, f32[256,256]{1,0:T(8,128)S(1)}, u32[]{:S(2)}, u32[]{:S(2)}) collective-permute-start(f32[256,256]{1,0:T(8,128)S(1)} %fusion.28), channel_id=1, source_target_pairs={{0,1},{1,2},{2,3},{3,4},{4,5},{5,6},{6,7},{7,8},{8,9},{9,10},{10,1... | collective-permute-start | bytes 786440 | tf_op jit(solution)/shard_map/ppermute | solution.py:21
  116.8 10.0 %copy-start.10 = (bf16[1,1,1,512,256]{4,3,2,1,0:T(8,128)(2,1)S(1)}, bf16[1,1,1,512,256]{4,3,2,1,0:T(8,128)(2,1)}, u32[]{:S(2)}) copy-start(bf16[1,1,1,512,256]{4,3,2,1,0:T(8,128)(2,1)} %get-tuple-element.15) | copy-start | bytes 786436
  116.9 10.0 %collective-permute-start.11 = (f32[256,256]{1,0:T(8,128)S(1)}, f32[256,256]{1,0:T(8,128)S(1)}, u32[]{:S(2)}, u32[]{:S(2)}) collective-permute-start(f32[256,256]{1,0:T(8,128)S(1)} %fusion.24), channel_id=1, source_target_pairs={{0,1},{1,2},{2,3},{3,4},{4,5},{5,6},{6,7},{7,8},{8,9},{9,10},{10,1... | collective-permute-start | bytes 786440 | tf_op jit(solution)/shard_map/ppermute | solution.py:21
  129.3 10.0 %copy-start.9 = (bf16[1,1,1,512,256]{4,3,2,1,0:T(8,128)(2,1)S(1)}, bf16[1,1,1,512,256]{4,3,2,1,0:T(8,128)(2,1)}, u32[]{:S(2)}) copy-start(bf16[1,1,1,512,256]{4,3,2,1,0:T(8,128)(2,1)} %get-tuple-element.21) | copy-start | bytes 786436
  129.4 10.0 %collective-permute-start.12 = (f32[256,256]{1,0:T(8,128)S(1)}, f32[256,256]{1,0:T(8,128)S(1)}, u32[]{:S(2)}, u32[]{:S(2)}) collective-permute-start(f32[256,256]{1,0:T(8,128)S(1)} %fusion.20), channel_id=1, source_target_pairs={{0,1},{1,2},{2,3},{3,4},{4,5},{5,6},{6,7},{7,8},{8,9},{9,10},{10,1... | collective-permute-start | bytes 786440 | tf_op jit(solution)/shard_map/ppermute | solution.py:21
  141.9 9.8 %collective-permute-start.13 = (f32[256,256]{1,0:T(8,128)S(1)}, f32[256,256]{1,0:T(8,128)S(1)}, u32[]{:S(2)}, u32[]{:S(2)}) collective-permute-start(f32[256,256]{1,0:T(8,128)S(1)} %fusion.16), channel_id=1, source_target_pairs={{0,1},{1,2},{2,3},{3,4},{4,5},{5,6},{6,7},{7,8},{8,9},{9,10},{10,1... | collective-permute-start | bytes 786440 | tf_op jit(solution)/shard_map/ppermute | solution.py:21
  (8 other events, 27.7 us)

commit v4 on v1

--- a/solution.py
+++ b/solution.py
@@ -51,8 +51,11 @@
         mixings.append(
             jnp.sum(jnp.where(picked[:, None, None, None], tile_collection, 0.0), axis=0)
         )
-    stacked = jnp.stack(neighbours).reshape(len(sources), sub_count, TILE, rank_width)
-    total_sum = jnp.einsum("bgcj,bgjz->gcz", jnp.stack(mixings), stacked, precision=STEP)
+    stacked = jnp.concatenate(
+        [n.reshape(sub_count, TILE, rank_width) for n in neighbours], axis=1
+    )
+    mixing = jnp.concatenate(mixings, axis=2)
+    total_sum = jnp.einsum("gck,gkz->gcz", mixing, stacked, precision=STEP)
     return total_sum.reshape(user_rows, rank_width) / count_used.astype(jnp.float32)
 
 

time: 137 us -> 137 us (level)
  no operation moved by 1% of the time
where the time goes in v4:
time: 137 us; the launch traced here: 136 us
  waiting for transfers between devices  58.2 us (42%)
  matrix products  33.2 us (24%)
  between operations  22.8 us (17%)
  starting transfers between devices  10.9 us (8%)
  local copies, waits for them, and re-layouts  9.62 us (7%)
    ppermute x11, waiting for transfers between devices, passed_along(): return lax.ppermute(value, axis, pairs)  58.2 us
    dot_general x32, matrix products, chain_part(): lax.dot_general(residual_err, block_rows, (((0,), (0,)), ((), ())), preci...  11.4 us
    ppermute x11, starting transfers between devices, passed_along(): return lax.ppermute(value, axis, pairs)  10.9 us
    dot_general x32, matrix products, chain_part(): lax.dot_general(block_rows, part, (((1,), (1,)), ((), ())), precision=STEP)  10.7 us
    dot_general x32, matrix products, shards(): grad_users = grad_users + jnp.dot(errors[c][k], held[c][k], precision=STEP)  8.66 us
    slice x1, local copies, waits for them, and re-layouts, shards(): stop_ratings = ratings[0, 0, stop_num]  2.9 us
  transfers between devices with their start and end apart: 11, of which 6 were waited for; matrix products, arithmetic and copies ran while one was open for 17% of the time, Pallas kernels for 0%

profile of v4, /device:TPU:0, one launch (start us, length us, event | category | flops | bytes accessed | tf_op | source)
XLA Modules:
  0.0 136.0 jit_solution(5225980411254449188)
XLA Ops:
  0.6 3.6 %collective-permute-start.3 = (f32[512,256]{1,0:T(8,128)}, f32[512,256]{1,0:T(8,128)}, u32[]{:S(2)}, u32[]{:S(2)}) collective-permute-start(f32[512,256]{1,0:T(8,128)} %bitcast.439), channel_id=1, source_target_pairs={{0,240},{16,0},{32,16},{48,32},{64,48},{80,64},{96,80},{112,96},{1... | collective-permute-start | bytes 1572872 | tf_op jit(solution)/shard_map/ppermute | solution.py:21
  4.2 3.4 %collective-permute-start = (f32[512,256]{1,0:T(8,128)}, f32[512,256]{1,0:T(8,128)}, u32[]{:S(2)}, u32[]{:S(2)}) collective-permute-start(f32[512,256]{1,0:T(8,128)} %bitcast.442), channel_id=1, source_target_pairs={{0,128},{16,144},{32,160},{48,176},{64,192},{80,208},{96,224},{112... | collective-permute-start | bytes 1572872 | tf_op jit(solution)/shard_map/ppermute | solution.py:21
  7.6 1.8 %fusion.329 = (s32[1,1]{0,1:T(1,128)}, s32[1,1]{0,1:T(1,128)}, s32[1,1]{0,1:T(1,128)}, s32[1,1]{0,1:T(1,128)}, s32[1,1]{0,1:T(1,128)}, /*index=5*/s32[1,1]{0,1:T...) fusion(s32[8,4]{0,1:T(4,128)} %param.15), kind=kLoop, calls=%fused_computation.437 | loop fusion | bytes 104 | tf_op jit(solution)/shard_map/slice | solution.py:84
  12.1 2.9 %fusion.327 = (bf16[1,1,1,512,256]{4,3,2,1,0:T(8,128)(2,1)}, bf16[1,1,1,512,256]{4,3,2,1,0:T(8,128)(2,1)}, bf16[1,1,1,512,256]{4,3,2,1,0:T(8,128)(2,1)}, bf16[1,...) fusion(bf16[1,1,8,512,256]{4,3,2,1,0:T(8,128)(2,1)} %param.10), kind=kLoop, calls=%fused_computation.435 | loop fusion | bytes 4194304 | tf_op jit(solution)/shard_map/slice | solution.py:82
  15.0 0.4 copy-done.1
  15.3 1.5 %fusion.326 = (s32[1,1,1,512,256]{4,3,2,1,0:T(8,128)S(1)}, s32[1,1,1,512,256]{4,3,2,1,0:T(8,128)}, s32[1,1,1,512,256]{4,3,2,1,0:T(8,128)}, s32[1,1,1,512,256]{4,...) fusion(s32[1,1,8,512,256]{4,3,2,1,0:T(8,128)S(1)} %copy-done.1), kind=kLoop, calls=%fused_computation.434 | loop fusion | bytes 8388608 | tf_op jit(solution)/shard_map/slice | solution.py:83
  19.0 1.2 fusion.160
  20.2 1.0 fusion.37
  21.3 1.5 %collective-permute-start.4 = (f32[256,256]{1,0:T(8,128)}, f32[256,256]{1,0:T(8,128)S(1)}, u32[]{:S(2)}, u32[]{:S(2)}) collective-permute-start(f32[256,256]{1,0:T(8,128)} %fusion.37), channel_id=1, source_target_pairs={{0,1},{1,2},{2,3},{3,4},{4,5},{5,6},{6,7},{7,8},{8,9},{9,10},{10,1... | collective-permute-start | bytes 786440 | tf_op jit(solution)/shard_map/ppermute | solution.py:21
  23.7 1.2 fusion.167
  24.9 1.3 fusion.183
  26.2 0.7 fusion.328
  45.3 2.5 %fusion.173 = f32[4,128,256]{2,1,0:T(8,128)S(1)} fusion(f32[4,128,256]{2,1,0:T(8,128)} %bitcast.27, f32[4,128,256]{2,1,0:T(8,128)} %bitcast.26, f32[4,128,256]{2,1,0:T(8,128)} %bitcast.25, f32[4,128,256]{2,1,0:T(8,128)} %bitcast.24, f32[4,128,128]{2,1,0:T(8,128)} %get-tuple-element.5, f32[4,128,128]{2,1,0:T(8,128)} %get-tuple-element.4, ...), kind=kOutput, calls=%fused_computation.269 | convolution fusion | flops 405143552 | bytes 3670020 | tf_op jit(solution)/shard_map/gck,gkz->gcz/dot_general | solution.py:58
  47.9 0.9 copy-done.7
  49.2 0.3 fusion.36
  51.4 1.6 %collective-permute-start.5 = (f32[256,256]{1,0:T(8,128)S(1)}, f32[256,256]{1,0:T(8,128)S(1)}, u32[]{:S(2)}, u32[]{:S(2)}) collective-permute-start(f32[256,256]{1,0:T(8,128)S(1)} %fusion.33), channel_id=1, source_target_pairs={{0,1},{1,2},{2,3},{3,4},{4,5},{5,6},{6,7},{7,8},{8,9},{9,10},{10,1... | collective-permute-start | bytes 786440 | tf_op jit(solution)/shard_map/ppermute | solution.py:21
  54.0 8.0 %collective-permute-done.5 = f32[256,256]{1,0:T(8,128)S(1)} collective-permute-done((f32[256,256]{1,0:T(8,128)S(1)}, f32[256,256]{1,0:T(8,128)S(1)}, u32[]{:S(2)}, u32[]{:S(2)}) %collective-permute-start.5) | collective-permute-done | bytes 262176 | tf_op jit(solution)/shard_map/ppermute | solution.py:21
  65.9 10.7 %collective-permute-done.6 = f32[256,256]{1,0:T(8,128)S(1)} collective-permute-done((f32[256,256]{1,0:T(8,128)S(1)}, f32[256,256]{1,0:T(8,128)S(1)}, u32[]{:S(2)}, u32[]{:S(2)}) %collective-permute-start.6) | collective-permute-done | bytes 262176 | tf_op jit(solution)/shard_map/ppermute | solution.py:21
  80.3 11.1 %collective-permute-done.7 = f32[256,256]{1,0:T(8,128)S(1)} collective-permute-done((f32[256,256]{1,0:T(8,128)S(1)}, f32[256,256]{1,0:T(8,128)S(1)}, u32[]{:S(2)}, u32[]{:S(2)}) %collective-permute-start.7) | collective-permute-done | bytes 262176 | tf_op jit(solution)/shard_map/ppermute | solution.py:21
  95.0 10.3 %collective-permute-done.8 = f32[256,256]{1,0:T(8,128)S(1)} collective-permute-done((f32[256,256]{1,0:T(8,128)S(1)}, f32[256,256]{1,0:T(8,128)S(1)}, u32[]{:S(2)}, u32[]{:S(2)}) %collective-permute-start.8) | collective-permute-done | bytes 262176 | tf_op jit(solution)/shard_map/ppermute | solution.py:21
  109.2 9.4 %collective-permute-done.9 = f32[256,256]{1,0:T(8,128)S(1)} collective-permute-done((f32[256,256]{1,0:T(8,128)S(1)}, f32[256,256]{1,0:T(8,128)S(1)}, u32[]{:S(2)}, u32[]{:S(2)}) %collective-permute-start.9) | collective-permute-done | bytes 262176 | tf_op jit(solution)/shard_map/ppermute | solution.py:21
  122.3 8.6 %collective-permute-done.10 = f32[256,256]{1,0:T(8,128)S(1)} collective-permute-done((f32[256,256]{1,0:T(8,128)S(1)}, f32[256,256]{1,0:T(8,128)S(1)}, u32[]{:S(2)}, u32[]{:S(2)}) %collective-permute-start.10) | collective-permute-done | bytes 262176 | tf_op jit(solution)/shard_map/ppermute | solution.py:21
  133.2 1.0 fusion.9
  135.2 0.8 copy-done.22
  (160 shorter events, 27.4 us)
Async XLA Ops:
  0.6 44.6 %collective-permute-start.3 = (f32[512,256]{1,0:T(8,128)}, f32[512,256]{1,0:T(8,128)}, u32[]{:S(2)}, u32[]{:S(2)}) collective-permute-start(f32[512,256]{1,0:T(8,128)} %bitcast.439), channel_id=1, source_target_pairs={{0,240},{16,0},{32,16},{48,32},{64,48},{80,64},{96,80},{112,96},{1... | collective-permute-start | bytes 1572872 | tf_op jit(solution)/shard_map/ppermute | solution.py:21
  4.2 41.0 %collective-permute-start.2 = (f32[512,256]{1,0:T(8,128)}, f32[512,256]{1,0:T(8,128)}, u32[]{:S(2)}, u32[]{:S(2)}) collective-permute-start(f32[512,256]{1,0:T(8,128)} %bitcast.440), channel_id=1, source_target_pairs={{0,16},{16,32},{32,48},{48,64},{64,80},{80,96},{96,112},{112,128},... | collective-permute-start | bytes 1572872 | tf_op jit(solution)/shard_map/ppermute | solution.py:21
  4.2 41.0 %collective-permute-start.1 = (f32[512,256]{1,0:T(8,128)}, f32[512,256]{1,0:T(8,128)}, u32[]{:S(2)}, u32[]{:S(2)}) collective-permute-start(f32[512,256]{1,0:T(8,128)} %bitcast.441), channel_id=1, source_target_pairs={{0,32},{16,48},{32,64},{48,80},{64,96},{80,112},{96,128},{112,144}... | collective-permute-start | bytes 1572872 | tf_op jit(solution)/shard_map/ppermute | solution.py:21
  4.2 41.0 %collective-permute-start = (f32[512,256]{1,0:T(8,128)}, f32[512,256]{1,0:T(8,128)}, u32[]{:S(2)}, u32[]{:S(2)}) collective-permute-start(f32[512,256]{1,0:T(8,128)} %bitcast.442), channel_id=1, source_target_pairs={{0,128},{16,144},{32,160},{48,176},{64,192},{80,208},{96,224},{112... | collective-permute-start | bytes 1572872 | tf_op jit(solution)/shard_map/ppermute | solution.py:21
  18.9 6.0 %copy-start.24 = (s32[1,1,4]{2,1,0:T(1,128)S(1)}, s32[1,1,4]{2,1,0:T(1,128)}, u32[]{:S(2)}) copy-start(s32[1,1,4]{2,1,0:T(1,128)} %param.12) | copy-start | bytes 52
  19.0 6.0 %copy-start.13 = (f32[1,1,4,4,128,128]{5,4,3,2,1,0:T(8,128)S(1)}, f32[1,1,4,4,128,128]{5,4,3,2,1,0:T(8,128)}, u32[]{:S(2)}) copy-start(f32[1,1,4,4,128,128]{5,4,3,2,1,0:T(8,128)} %param.14) | copy-start | bytes 3145732
  21.3 26.7 %collective-permute-start.4 = (f32[256,256]{1,0:T(8,128)}, f32[256,256]{1,0:T(8,128)S(1)}, u32[]{:S(2)}, u32[]{:S(2)}) collective-permute-start(f32[256,256]{1,0:T(8,128)} %fusion.37), channel_id=1, source_target_pairs={{0,1},{1,2},{2,3},{3,4},{4,5},{5,6},{6,7},{7,8},{8,9},{9,10},{10,1... | collective-permute-start | bytes 786440 | tf_op jit(solution)/shard_map/ppermute | solution.py:21
  23.7 21.3 %copy-start.9 = (f32[128,256]{1,0:T(8,128)S(1)}, f32[128,256]{1,0:T(8,128)}, u32[]{:S(2)}) copy-start(f32[128,256]{1,0:T(8,128)} %copy-done.8) | copy-start | bytes 393220
  51.4 10.6 %collective-permute-start.5 = (f32[256,256]{1,0:T(8,128)S(1)}, f32[256,256]{1,0:T(8,128)S(1)}, u32[]{:S(2)}, u32[]{:S(2)}) collective-permute-start(f32[256,256]{1,0:T(8,128)S(1)} %fusion.33), channel_id=1, source_target_pairs={{0,1},{1,2},{2,3},{3,4},{4,5},{5,6},{6,7},{7,8},{8,9},{9,10},{10,1... | collective-permute-start | bytes 786440 | tf_op jit(solution)/shard_map/ppermute | solution.py:21
  53.0 9.1 %copy-start.6 = (s32[1,1,1,512,256]{4,3,2,1,0:T(8,128)S(1)}, s32[1,1,1,512,256]{4,3,2,1,0:T(8,128)}, u32[]{:S(2)}) copy-start(s32[1,1,1,512,256]{4,3,2,1,0:T(8,128)} %get-tuple-element.10) | copy-start | bytes 1572868
  53.0 9.1 %copy-start.19 = (bf16[1,1,1,512,256]{4,3,2,1,0:T(8,128)(2,1)S(1)}, bf16[1,1,1,512,256]{4,3,2,1,0:T(8,128)(2,1)}, u32[]{:S(2)}) copy-start(bf16[1,1,1,512,256]{4,3,2,1,0:T(8,128)(2,1)} %get-tuple-element.18) | copy-start | bytes 786436
  64.6 12.0 %copy-start.5 = (s32[1,1,1,512,256]{4,3,2,1,0:T(8,128)S(1)}, s32[1,1,1,512,256]{4,3,2,1,0:T(8,128)}, u32[]{:S(2)}) copy-start(s32[1,1,1,512,256]{4,3,2,1,0:T(8,128)} %get-tuple-element.9) | copy-start | bytes 1572868
  64.6 12.0 %copy-start.18 = (bf16[1,1,1,512,256]{4,3,2,1,0:T(8,128)(2,1)S(1)}, bf16[1,1,1,512,256]{4,3,2,1,0:T(8,128)(2,1)}, u32[]{:S(2)}) copy-start(bf16[1,1,1,512,256]{4,3,2,1,0:T(8,128)(2,1)} %get-tuple-element.17) | copy-start | bytes 786436
  64.6 12.0 %collective-permute-start.6 = (f32[256,256]{1,0:T(8,128)S(1)}, f32[256,256]{1,0:T(8,128)S(1)}, u32[]{:S(2)}, u32[]{:S(2)}) collective-permute-start(f32[256,256]{1,0:T(8,128)S(1)} %fusion.29), channel_id=1, source_target_pairs={{0,1},{1,2},{2,3},{3,4},{4,5},{5,6},{6,7},{7,8},{8,9},{9,10},{10,1... | collective-permute-start | bytes 786440 | tf_op jit(solution)/shard_map/ppermute | solution.py:21
  79.1 12.2 %copy-start.4 = (s32[1,1,1,512,256]{4,3,2,1,0:T(8,128)S(1)}, s32[1,1,1,512,256]{4,3,2,1,0:T(8,128)}, u32[]{:S(2)}) copy-start(s32[1,1,1,512,256]{4,3,2,1,0:T(8,128)} %get-tuple-element.8) | copy-start | bytes 1572868
  79.1 12.2 %copy-start.17 = (bf16[1,1,1,512,256]{4,3,2,1,0:T(8,128)(2,1)S(1)}, bf16[1,1,1,512,256]{4,3,2,1,0:T(8,128)(2,1)}, u32[]{:S(2)}) copy-start(bf16[1,1,1,512,256]{4,3,2,1,0:T(8,128)(2,1)} %get-tuple-element.16) | copy-start | bytes 786436
  79.1 12.2 %collective-permute-start.7 = (f32[256,256]{1,0:T(8,128)S(1)}, f32[256,256]{1,0:T(8,128)S(1)}, u32[]{:S(2)}, u32[]{:S(2)}) collective-permute-start(f32[256,256]{1,0:T(8,128)S(1)} %fusion.25), channel_id=1, source_target_pairs={{0,1},{1,2},{2,3},{3,4},{4,5},{5,6},{6,7},{7,8},{8,9},{9,10},{10,1... | collective-permute-start | bytes 786440 | tf_op jit(solution)/shard_map/ppermute | solution.py:21
  93.9 11.5 %copy-start.3 = (s32[1,1,1,512,256]{4,3,2,1,0:T(8,128)S(1)}, s32[1,1,1,512,256]{4,3,2,1,0:T(8,128)}, u32[]{:S(2)}) copy-start(s32[1,1,1,512,256]{4,3,2,1,0:T(8,128)} %get-tuple-element.7) | copy-start | bytes 1572868
  93.9 11.5 %copy-start.16 = (bf16[1,1,1,512,256]{4,3,2,1,0:T(8,128)(2,1)S(1)}, bf16[1,1,1,512,256]{4,3,2,1,0:T(8,128)(2,1)}, u32[]{:S(2)}) copy-start(bf16[1,1,1,512,256]{4,3,2,1,0:T(8,128)(2,1)} %get-tuple-element.15) | copy-start | bytes 786436
  93.9 11.4 %collective-permute-start.8 = (f32[256,256]{1,0:T(8,128)S(1)}, f32[256,256]{1,0:T(8,128)S(1)}, u32[]{:S(2)}, u32[]{:S(2)}) collective-permute-start(f32[256,256]{1,0:T(8,128)S(1)} %fusion.21), channel_id=1, source_target_pairs={{0,1},{1,2},{2,3},{3,4},{4,5},{5,6},{6,7},{7,8},{8,9},{9,10},{10,1... | collective-permute-start | bytes 786440 | tf_op jit(solution)/shard_map/ppermute | solution.py:21
  107.9 10.8 %copy-start.15 = (bf16[1,1,1,512,256]{4,3,2,1,0:T(8,128)(2,1)S(1)}, bf16[1,1,1,512,256]{4,3,2,1,0:T(8,128)(2,1)}, u32[]{:S(2)}) copy-start(bf16[1,1,1,512,256]{4,3,2,1,0:T(8,128)(2,1)} %get-tuple-element.21) | copy-start | bytes 786436
  107.9 10.8 %collective-permute-start.9 = (f32[256,256]{1,0:T(8,128)S(1)}, f32[256,256]{1,0:T(8,128)S(1)}, u32[]{:S(2)}, u32[]{:S(2)}) collective-permute-start(f32[256,256]{1,0:T(8,128)S(1)} %fusion.17), channel_id=1, source_target_pairs={{0,1},{1,2},{2,3},{3,4},{4,5},{5,6},{6,7},{7,8},{8,9},{9,10},{10,1... | collective-permute-start | bytes 786440 | tf_op jit(solution)/shard_map/ppermute | solution.py:21
  121.2 9.8 %copy-start.14 = (bf16[1,1,1,512,256]{4,3,2,1,0:T(8,128)(2,1)S(1)}, bf16[1,1,1,512,256]{4,3,2,1,0:T(8,128)(2,1)}, u32[]{:S(2)}) copy-start(bf16[1,1,1,512,256]{4,3,2,1,0:T(8,128)(2,1)} %get-tuple-element.14) | copy-start | bytes 786436
  121.2 9.8 %collective-permute-start.10 = (f32[256,256]{1,0:T(8,128)S(1)}, f32[256,256]{1,0:T(8,128)S(1)}, u32[]{:S(2)}, u32[]{:S(2)}) collective-permute-start(f32[256,256]{1,0:T(8,128)S(1)} %fusion.13), channel_id=1, source_target_pairs={{0,1},{1,2},{2,3},{3,4},{4,5},{5,6},{6,7},{7,8},{8,9},{9,10},{10,1... | collective-permute-start | bytes 786440 | tf_op jit(solution)/shard_map/ppermute | solution.py:21
  (12 other events, 27.8 us)

commit v5 on v1

--- a/solution.py
+++ b/solution.py
@@ -79,7 +79,14 @@
         stop_ratings = ratings[0, 0, stop_num]
         halting_mask = rated_mask[0, 0, stop_num]
         starts = [plan[stop_num, k] * TILE for k in range(sub_count)]
-        rows = [lax.dynamic_slice_in_dim(user_now, s, TILE, 0) for s in starts]
+        if stop_num == 1:
+            rows = [
+                lax.dynamic_slice_in_dim(goal_free, s, TILE, 0)
+                + (learning_rate * graph_weight) * lax.dynamic_slice_in_dim(target, s, TILE, 0)
+                for s in starts
+            ]
+        else:
+            rows = [lax.dynamic_slice_in_dim(user_now, s, TILE, 0) for s in starts]
         last = stop_num == STOPS - 1
         errors = []
         held = []
@@ -104,6 +111,7 @@
                 user_now, block_rows - learning_rate * grad_users, starts[k], 0
             )
         if stop_num == 0:
+            goal_free = user_now
             user_now = user_now + (learning_rate * graph_weight) * target
     item_now = jnp.concatenate(parts, axis=0)
     return (user_now[None, None], item_now[None, None])

time: 137 us -> 136 us (level)
  no operation moved by 1% of the time
where the time goes in v5:
time: 136 us; the launch traced here: 135 us
  waiting for transfers between devices  57.9 us (43%)
  matrix products  33.3 us (24%)
  between operations  22.8 us (17%)
  starting transfers between devices  10.9 us (8%)
  local copies, waits for them, and re-layouts  9.28 us (7%)
  other arithmetic  1.36 us (1%)
    ppermute x11, waiting for transfers between devices, passed_along(): return lax.ppermute(value, axis, pairs)  57.9 us
    dot_general x32, matrix products, chain_part(): lax.dot_general(residual_err, block_rows, (((0,), (0,)), ((), ())), preci...  11.4 us
    ppermute x11, starting transfers between devices, passed_along(): return lax.ppermute(value, axis, pairs)  10.9 us
    dot_general x32, matrix products, chain_part(): lax.dot_general(block_rows, part, (((1,), (1,)), ((), ())), precision=STEP)  10.7 us
    dot_general x32, matrix products, shards(): grad_users = grad_users + jnp.dot(errors[c][k], held[c][k], precision=STEP)  8.67 us
    slice x1, local copies, waits for them, and re-layouts, shards(): stop_ratings = ratings[0, 0, stop_num]  2.9 us
  transfers between devices with their start and end apart: 11, of which 6 were waited for; matrix products, arithmetic and copies ran while one was open for 17% of the time, Pallas kernels for 0%

profile of v5, /device:TPU:0, one launch (start us, length us, event | category | flops | bytes accessed | tf_op | source)
XLA Modules:
  0.0 135.5 jit_solution(15500237314139435466)
XLA Ops:
  0.6 3.6 %collective-permute-start.3 = (f32[512,256]{1,0:T(8,128)}, f32[512,256]{1,0:T(8,128)}, u32[]{:S(2)}, u32[]{:S(2)}) collective-permute-start(f32[512,256]{1,0:T(8,128)} %bitcast.464), channel_id=1, source_target_pairs={{0,240},{16,0},{32,16},{48,32},{64,48},{80,64},{96,80},{112,96},{1... | collective-permute-start | bytes 1572872 | tf_op jit(solution)/shard_map/ppermute | solution.py:21
  4.2 3.4 %collective-permute-start = (f32[512,256]{1,0:T(8,128)}, f32[512,256]{1,0:T(8,128)}, u32[]{:S(2)}, u32[]{:S(2)}) collective-permute-start(f32[512,256]{1,0:T(8,128)} %bitcast.467), channel_id=1, source_target_pairs={{0,128},{16,144},{32,160},{48,176},{64,192},{80,208},{96,224},{112... | collective-permute-start | bytes 1572872 | tf_op jit(solution)/shard_map/ppermute | solution.py:21
  7.6 1.8 %fusion.318 = (s32[1,1]{0,1:T(1,128)}, s32[1,1]{0,1:T(1,128)}, s32[1,1]{0,1:T(1,128)}, s32[1,1]{0,1:T(1,128)}, s32[1,1]{0,1:T(1,128)}, /*index=5*/s32[1,1]{0,1:T...) fusion(s32[8,4]{0,1:T(4,128)} %param.15), kind=kLoop, calls=%fused_computation.426 | loop fusion | bytes 104 | tf_op jit(solution)/shard_map/slice | solution.py:81
  12.1 2.9 %fusion.316 = (bf16[1,1,1,512,256]{4,3,2,1,0:T(8,128)(2,1)}, bf16[1,1,1,512,256]{4,3,2,1,0:T(8,128)(2,1)}, bf16[1,1,1,512,256]{4,3,2,1,0:T(8,128)(2,1)}, bf16[1,...) fusion(bf16[1,1,8,512,256]{4,3,2,1,0:T(8,128)(2,1)} %param.10), kind=kLoop, calls=%fused_computation.424 | loop fusion | bytes 4194304 | tf_op jit(solution)/shard_map/slice | solution.py:79
  15.0 0.4 copy-done.1
  15.3 1.5 %fusion.315 = (s32[1,1,1,512,256]{4,3,2,1,0:T(8,128)S(1)}, s32[1,1,1,512,256]{4,3,2,1,0:T(8,128)}, s32[1,1,1,512,256]{4,3,2,1,0:T(8,128)}, s32[1,1,1,512,256]{4,...) fusion(s32[1,1,8,512,256]{4,3,2,1,0:T(8,128)S(1)} %copy-done.1), kind=kLoop, calls=%fused_computation.423 | loop fusion | bytes 8388608 | tf_op jit(solution)/shard_map/slice | solution.py:80
  19.0 1.2 fusion.163
  20.2 0.6 copy-done.8
  20.9 1.0 fusion.40
  21.9 1.5 %collective-permute-start.4 = (f32[256,256]{1,0:T(8,128)}, f32[256,256]{1,0:T(8,128)S(1)}, u32[]{:S(2)}, u32[]{:S(2)}) collective-permute-start(f32[256,256]{1,0:T(8,128)} %fusion.40), channel_id=1, source_target_pairs={{0,1},{1,2},{2,3},{3,4},{4,5},{5,6},{6,7},{7,8},{8,9},{9,10},{10,1... | collective-permute-start | bytes 786440 | tf_op jit(solution)/shard_map/ppermute | solution.py:21
  24.4 1.2 fusion.170
  25.6 1.3 fusion.183
  26.9 0.7 fusion.317
  45.9 2.6 %fusion.187 = f32[4,128,256]{2,1,0:T(8,128)S(1)} fusion(f32[1,4,128,256]{3,2,0,1:T(8,128)} %bitcast.35, f32[1,4,128,256]{3,2,0,1:T(8,128)} %bitcast.33, f32[1,4,128,256]{3,2,0,1:T(8,128)} %bitcast.31, f32[1,4,128,256]{3,2,0,1:T(8,128)} %bitcast.29, f32[1,4,128,128]{3,2,0,1:T(8,128)} %bitcast.472, f32[1,4,128,128]{3,2,0,1:T(8,128)} %bitcast.471, ...), kind=kOutput, calls=%fused_computation.286 | convolution fusion | flops 405143552 | bytes 3670020 | tf_op jit(solution)/shard_map/bgcj,bgjz->gcz/dot_general | solution.py:55
  50.9 0.3 fusion.36
  51.2 1.6 %collective-permute-start.5 = (f32[256,256]{1,0:T(8,128)S(1)}, f32[256,256]{1,0:T(8,128)S(1)}, u32[]{:S(2)}, u32[]{:S(2)}) collective-permute-start(f32[256,256]{1,0:T(8,128)S(1)} %fusion.36), channel_id=1, source_target_pairs={{0,1},{1,2},{2,3},{3,4},{4,5},{5,6},{6,7},{7,8},{8,9},{9,10},{10,1... | collective-permute-start | bytes 786440 | tf_op jit(solution)/shard_map/ppermute | solution.py:21
  53.8 8.7 %collective-permute-done.5 = f32[256,256]{1,0:T(8,128)S(1)} collective-permute-done((f32[256,256]{1,0:T(8,128)S(1)}, f32[256,256]{1,0:T(8,128)S(1)}, u32[]{:S(2)}, u32[]{:S(2)}) %collective-permute-start.5) | collective-permute-done | bytes 262176 | tf_op jit(solution)/shard_map/ppermute | solution.py:21
  66.4 11.3 %collective-permute-done.6 = f32[256,256]{1,0:T(8,128)S(1)} collective-permute-done((f32[256,256]{1,0:T(8,128)S(1)}, f32[256,256]{1,0:T(8,128)S(1)}, u32[]{:S(2)}, u32[]{:S(2)}) %collective-permute-start.6) | collective-permute-done | bytes 262176 | tf_op jit(solution)/shard_map/ppermute | solution.py:21
  81.4 10.6 %collective-permute-done.7 = f32[256,256]{1,0:T(8,128)S(1)} collective-permute-done((f32[256,256]{1,0:T(8,128)S(1)}, f32[256,256]{1,0:T(8,128)S(1)}, u32[]{:S(2)}, u32[]{:S(2)}) %collective-permute-start.7) | collective-permute-done | bytes 262176 | tf_op jit(solution)/shard_map/ppermute | solution.py:21
  95.7 9.8 %collective-permute-done.8 = f32[256,256]{1,0:T(8,128)S(1)} collective-permute-done((f32[256,256]{1,0:T(8,128)S(1)}, f32[256,256]{1,0:T(8,128)S(1)}, u32[]{:S(2)}, u32[]{:S(2)}) %collective-permute-start.8) | collective-permute-done | bytes 262176 | tf_op jit(solution)/shard_map/ppermute | solution.py:21
  109.3 8.8 %collective-permute-done.9 = f32[256,256]{1,0:T(8,128)S(1)} collective-permute-done((f32[256,256]{1,0:T(8,128)S(1)}, f32[256,256]{1,0:T(8,128)S(1)}, u32[]{:S(2)}, u32[]{:S(2)}) %collective-permute-start.9) | collective-permute-done | bytes 262176 | tf_op jit(solution)/shard_map/ppermute | solution.py:21
  121.8 8.6 %collective-permute-done.10 = f32[256,256]{1,0:T(8,128)S(1)} collective-permute-done((f32[256,256]{1,0:T(8,128)S(1)}, f32[256,256]{1,0:T(8,128)S(1)}, u32[]{:S(2)}, u32[]{:S(2)}) %collective-permute-start.10) | collective-permute-done | bytes 262176 | tf_op jit(solution)/shard_map/ppermute | solution.py:21
  132.7 1.0 fusion.12
  134.7 0.8 copy-done.22
  (159 shorter events, 27.4 us)
Async XLA Ops:
  0.6 45.2 %collective-permute-start.3 = (f32[512,256]{1,0:T(8,128)}, f32[512,256]{1,0:T(8,128)}, u32[]{:S(2)}, u32[]{:S(2)}) collective-permute-start(f32[512,256]{1,0:T(8,128)} %bitcast.464), channel_id=1, source_target_pairs={{0,240},{16,0},{32,16},{48,32},{64,48},{80,64},{96,80},{112,96},{1... | collective-permute-start | bytes 1572872 | tf_op jit(solution)/shard_map/ppermute | solution.py:21
  4.2 41.7 %collective-permute-start.2 = (f32[512,256]{1,0:T(8,128)}, f32[512,256]{1,0:T(8,128)}, u32[]{:S(2)}, u32[]{:S(2)}) collective-permute-start(f32[512,256]{1,0:T(8,128)} %bitcast.465), channel_id=1, source_target_pairs={{0,16},{16,32},{32,48},{48,64},{64,80},{80,96},{96,112},{112,128},... | collective-permute-start | bytes 1572872 | tf_op jit(solution)/shard_map/ppermute | solution.py:21
  4.2 41.7 %collective-permute-start.1 = (f32[512,256]{1,0:T(8,128)}, f32[512,256]{1,0:T(8,128)}, u32[]{:S(2)}, u32[]{:S(2)}) collective-permute-start(f32[512,256]{1,0:T(8,128)} %bitcast.466), channel_id=1, source_target_pairs={{0,32},{16,48},{32,64},{48,80},{64,96},{80,112},{96,128},{112,144}... | collective-permute-start | bytes 1572872 | tf_op jit(solution)/shard_map/ppermute | solution.py:21
  4.2 41.7 %collective-permute-start = (f32[512,256]{1,0:T(8,128)}, f32[512,256]{1,0:T(8,128)}, u32[]{:S(2)}, u32[]{:S(2)}) collective-permute-start(f32[512,256]{1,0:T(8,128)} %bitcast.467), channel_id=1, source_target_pairs={{0,128},{16,144},{32,160},{48,176},{64,192},{80,208},{96,224},{112... | collective-permute-start | bytes 1572872 | tf_op jit(solution)/shard_map/ppermute | solution.py:21
  18.9 6.6 %copy-start.24 = (s32[1,1,4]{2,1,0:T(1,128)S(1)}, s32[1,1,4]{2,1,0:T(1,128)}, u32[]{:S(2)}) copy-start(s32[1,1,4]{2,1,0:T(1,128)} %param.12) | copy-start | bytes 52
  19.0 6.6 %copy-start.13 = (f32[1,1,4,4,128,128]{5,4,3,2,1,0:T(8,128)S(1)}, f32[1,1,4,4,128,128]{5,4,3,2,1,0:T(8,128)}, u32[]{:S(2)}) copy-start(f32[1,1,4,4,128,128]{5,4,3,2,1,0:T(8,128)} %param.14) | copy-start | bytes 3145732
  21.9 26.7 %collective-permute-start.4 = (f32[256,256]{1,0:T(8,128)}, f32[256,256]{1,0:T(8,128)S(1)}, u32[]{:S(2)}, u32[]{:S(2)}) collective-permute-start(f32[256,256]{1,0:T(8,128)} %fusion.40), channel_id=1, source_target_pairs={{0,1},{1,2},{2,3},{3,4},{4,5},{5,6},{6,7},{7,8},{8,9},{9,10},{10,1... | collective-permute-start | bytes 786440 | tf_op jit(solution)/shard_map/ppermute | solution.py:21
  24.3 21.3 %copy-start.9 = (f32[128,256]{1,0:T(8,128)S(1)}, f32[128,256]{1,0:T(8,128)}, u32[]{:S(2)}) copy-start(f32[128,256]{1,0:T(8,128)} %copy-done.8) | copy-start | bytes 393220
  51.2 11.3 %copy-start.6 = (s32[1,1,1,512,256]{4,3,2,1,0:T(8,128)S(1)}, s32[1,1,1,512,256]{4,3,2,1,0:T(8,128)}, u32[]{:S(2)}) copy-start(s32[1,1,1,512,256]{4,3,2,1,0:T(8,128)} %get-tuple-element.10) | copy-start | bytes 1572868
  51.2 11.3 %copy-start.19 = (bf16[1,1,1,512,256]{4,3,2,1,0:T(8,128)(2,1)S(1)}, bf16[1,1,1,512,256]{4,3,2,1,0:T(8,128)(2,1)}, u32[]{:S(2)}) copy-start(bf16[1,1,1,512,256]{4,3,2,1,0:T(8,128)(2,1)} %get-tuple-element.18) | copy-start | bytes 786436
  51.2 11.3 %collective-permute-start.5 = (f32[256,256]{1,0:T(8,128)S(1)}, f32[256,256]{1,0:T(8,128)S(1)}, u32[]{:S(2)}, u32[]{:S(2)}) collective-permute-start(f32[256,256]{1,0:T(8,128)S(1)} %fusion.36), channel_id=1, source_target_pairs={{0,1},{1,2},{2,3},{3,4},{4,5},{5,6},{6,7},{7,8},{8,9},{9,10},{10,1... | collective-permute-start | bytes 786440 | tf_op jit(solution)/shard_map/ppermute | solution.py:21
  65.1 12.7 %copy-start.5 = (s32[1,1,1,512,256]{4,3,2,1,0:T(8,128)S(1)}, s32[1,1,1,512,256]{4,3,2,1,0:T(8,128)}, u32[]{:S(2)}) copy-start(s32[1,1,1,512,256]{4,3,2,1,0:T(8,128)} %get-tuple-element.9) | copy-start | bytes 1572868
  65.1 12.6 %copy-start.18 = (bf16[1,1,1,512,256]{4,3,2,1,0:T(8,128)(2,1)S(1)}, bf16[1,1,1,512,256]{4,3,2,1,0:T(8,128)(2,1)}, u32[]{:S(2)}) copy-start(bf16[1,1,1,512,256]{4,3,2,1,0:T(8,128)(2,1)} %get-tuple-element.17) | copy-start | bytes 786436
  65.1 12.6 %collective-permute-start.6 = (f32[256,256]{1,0:T(8,128)S(1)}, f32[256,256]{1,0:T(8,128)S(1)}, u32[]{:S(2)}, u32[]{:S(2)}) collective-permute-start(f32[256,256]{1,0:T(8,128)S(1)} %fusion.32), channel_id=1, source_target_pairs={{0,1},{1,2},{2,3},{3,4},{4,5},{5,6},{6,7},{7,8},{8,9},{9,10},{10,1... | collective-permute-start | bytes 786440 | tf_op jit(solution)/shard_map/ppermute | solution.py:21
  80.2 11.7 %copy-start.4 = (s32[1,1,1,512,256]{4,3,2,1,0:T(8,128)S(1)}, s32[1,1,1,512,256]{4,3,2,1,0:T(8,128)}, u32[]{:S(2)}) copy-start(s32[1,1,1,512,256]{4,3,2,1,0:T(8,128)} %get-tuple-element.8) | copy-start | bytes 1572868
  80.2 11.7 %copy-start.17 = (bf16[1,1,1,512,256]{4,3,2,1,0:T(8,128)(2,1)S(1)}, bf16[1,1,1,512,256]{4,3,2,1,0:T(8,128)(2,1)}, u32[]{:S(2)}) copy-start(bf16[1,1,1,512,256]{4,3,2,1,0:T(8,128)(2,1)} %get-tuple-element.16) | copy-start | bytes 786436
  80.3 11.7 %collective-permute-start.7 = (f32[256,256]{1,0:T(8,128)S(1)}, f32[256,256]{1,0:T(8,128)S(1)}, u32[]{:S(2)}, u32[]{:S(2)}) collective-permute-start(f32[256,256]{1,0:T(8,128)S(1)} %fusion.28), channel_id=1, source_target_pairs={{0,1},{1,2},{2,3},{3,4},{4,5},{5,6},{6,7},{7,8},{8,9},{9,10},{10,1... | collective-permute-start | bytes 786440 | tf_op jit(solution)/shard_map/ppermute | solution.py:21
  94.5 10.9 %copy-start.3 = (s32[1,1,1,512,256]{4,3,2,1,0:T(8,128)S(1)}, s32[1,1,1,512,256]{4,3,2,1,0:T(8,128)}, u32[]{:S(2)}) copy-start(s32[1,1,1,512,256]{4,3,2,1,0:T(8,128)} %get-tuple-element.7) | copy-start | bytes 1572868
  94.5 10.9 %copy-start.16 = (bf16[1,1,1,512,256]{4,3,2,1,0:T(8,128)(2,1)S(1)}, bf16[1,1,1,512,256]{4,3,2,1,0:T(8,128)(2,1)}, u32[]{:S(2)}) copy-start(bf16[1,1,1,512,256]{4,3,2,1,0:T(8,128)(2,1)} %get-tuple-element.15) | copy-start | bytes 786436
  94.5 10.9 %collective-permute-start.8 = (f32[256,256]{1,0:T(8,128)S(1)}, f32[256,256]{1,0:T(8,128)S(1)}, u32[]{:S(2)}, u32[]{:S(2)}) collective-permute-start(f32[256,256]{1,0:T(8,128)S(1)} %fusion.24), channel_id=1, source_target_pairs={{0,1},{1,2},{2,3},{3,4},{4,5},{5,6},{6,7},{7,8},{8,9},{9,10},{10,1... | collective-permute-start | bytes 786440 | tf_op jit(solution)/shard_map/ppermute | solution.py:21
  108.0 10.2 %copy-start.15 = (bf16[1,1,1,512,256]{4,3,2,1,0:T(8,128)(2,1)S(1)}, bf16[1,1,1,512,256]{4,3,2,1,0:T(8,128)(2,1)}, u32[]{:S(2)}) copy-start(bf16[1,1,1,512,256]{4,3,2,1,0:T(8,128)(2,1)} %get-tuple-element.21) | copy-start | bytes 786436
  108.0 10.2 %collective-permute-start.9 = (f32[256,256]{1,0:T(8,128)S(1)}, f32[256,256]{1,0:T(8,128)S(1)}, u32[]{:S(2)}, u32[]{:S(2)}) collective-permute-start(f32[256,256]{1,0:T(8,128)S(1)} %fusion.20), channel_id=1, source_target_pairs={{0,1},{1,2},{2,3},{3,4},{4,5},{5,6},{6,7},{7,8},{8,9},{9,10},{10,1... | collective-permute-start | bytes 786440 | tf_op jit(solution)/shard_map/ppermute | solution.py:21
  120.7 9.8 %copy-start.14 = (bf16[1,1,1,512,256]{4,3,2,1,0:T(8,128)(2,1)S(1)}, bf16[1,1,1,512,256]{4,3,2,1,0:T(8,128)(2,1)}, u32[]{:S(2)}) copy-start(bf16[1,1,1,512,256]{4,3,2,1,0:T(8,128)(2,1)} %get-tuple-element.14) | copy-start | bytes 786436
  120.7 9.8 %collective-permute-start.10 = (f32[256,256]{1,0:T(8,128)S(1)}, f32[256,256]{1,0:T(8,128)S(1)}, u32[]{:S(2)}, u32[]{:S(2)}) collective-permute-start(f32[256,256]{1,0:T(8,128)S(1)} %fusion.16), channel_id=1, source_target_pairs={{0,1},{1,2},{2,3},{3,4},{4,5},{5,6},{6,7},{7,8},{8,9},{9,10},{10,1... | collective-permute-start | bytes 786440 | tf_op jit(solution)/shard_map/ppermute | solution.py:21
  (12 other events, 30.3 us)
